TPU v7x, 1024 devices: a whole 4x8x16 slice. The times are simulated.
1024 devices in a mesh: rep: 4 (over z_hi, core), fsdp: 256 (over y, z_lo, x).
Axes of the slice: x: 4, y: 8, z: 16 (z_hi: 2, z_lo: 8; z = z_hi * 8 + z_lo), core: 2. Of those that a mesh axis runs over, the one named last changes fastest.
Arguments:
- anchor: float32 [3584, 7168], P('fsdp'), may hold values from -6 to 6
- momentum: float32 [3584, 7168], P('fsdp', 'rep'), may hold values from -3 to 3
- inner_weight: float32 [4, 3584, 7168], P('rep', 'fsdp'), may hold values from -6 to 6
- first_moment: float32 [4, 3584, 7168], P('rep', 'fsdp'), may hold values from -2 to 2
- second_moment: float32 [4, 3584, 7168], P('rep', 'fsdp'), may hold values from 0.01 to 1
- grad_first: bfloat16 [4, 3584, 7168], P('rep', 'fsdp'), may hold values from -1100 to 1100
- grad_second: bfloat16 [4, 3584, 7168], P('rep', 'fsdp'), may hold values from -1100 to 1100
- outer_step: int32 [1], replicated, may hold values from 0 to 15
Outputs:
- next_anchor: float32 [3584, 7168], P('fsdp')
- next_momentum: float32 [3584, 7168], P('fsdp', 'rep')
- next_inner: float32 [4, 3584, 7168], P('rep', 'fsdp')
- next_first: float32 [4, 3584, 7168], P('rep', 'fsdp')
- next_second: float32 [4, 3584, 7168], P('rep', 'fsdp')
All inputs are finite; a program needn't handle non-finite values.
Results may differ from a plain program's by a relative error of at most 0.0003.
Values sent between devices are 32-bit elements; how exact they have to be, the bound alone decides.
No kernel may reach another device: no remote copies, remote signals or barrier semaphores. Data moves between devices by JAX's collectives and lax.ppermute only.
A program may use at most 32 MiB of HBM per device.

v0:
```python
import functools
import math

import jax
import jax.numpy as jnp
from jax import lax
from jax.sharding import Mesh
from jax.sharding import PartitionSpec as P

D = 3584
FF = 7168
FSDP = ("fsdp_0", "fsdp_1", "fsdp_2")


def split_up(x, dim, length):
    before, after = (x.shape[:dim], x.shape[dim + 1 :])
    return jnp.moveaxis(x.reshape(*before, length, -1, *after), dim, 0)


def summed_on_arrival(x, axis, dim):
    pieces = split_up(x, dim, lax.axis_size(axis))
    arrived = lax.all_to_all(pieces, axis, split_axis=0, concat_axis=0, tiled=True)
    return arrived.sum(axis=0)


def over_axes(x, axes):
    return functools.reduce(lax.psum, axes, x)


def adam_apply(weight, first_moment, second_moment, grad_full, square_sum, step_count):
    factor = jnp.minimum(1.0, 0.5 * math.sqrt(D * FF) / (jnp.sqrt(square_sum) + 1e-06))
    scaled = factor * grad_full
    first_moment = 0.9 * first_moment + 0.1 * scaled
    second_moment = 0.95 * second_moment + 0.05 * scaled * scaled
    first_hat = first_moment / (1.0 - jnp.power(jnp.float32(0.9), step_count))
    second_hat = second_moment / (1.0 - jnp.power(jnp.float32(0.95), step_count))
    weight = weight - 0.1 * (first_hat / (jnp.sqrt(second_hat) + 1e-08) + 0.1 * weight)
    return (weight, first_moment, second_moment)


def outer_update(anchor, momentum, inner_weight):
    replicas = lax.axis_size("rep")
    col_count = momentum.shape[1]
    col_start = lax.axis_index("rep") * col_count
    pseudo = anchor - inner_weight[0]
    delta_share = summed_on_arrival(pseudo, "rep", 1)
    outer_grad = delta_share / replicas
    next_momentum = 0.9 * momentum + outer_grad
    anchor_share = lax.dynamic_slice_in_dim(anchor, col_start, col_count, 1)
    anchor_share = anchor_share - 0.7 * (outer_grad + 0.9 * next_momentum)
    next_anchor = lax.all_gather(anchor_share, "rep", axis=1, tiled=True)
    return (next_anchor, next_momentum)


def inner_steps(inner_weight, first_moment, second_moment, grad_first, grad_second, outer_step):
    base_step = 2 * outer_step[0]
    grad_one = grad_first[0].astype(jnp.float32)
    grad_two = grad_second[0].astype(jnp.float32)
    norm_one, norm_two = (
        over_axes(jnp.sum(grad_one * grad_one), FSDP),
        over_axes(jnp.sum(grad_two * grad_two), FSDP),
    )
    weight, moment_one, moment_two = adam_apply(
        inner_weight[0],
        first_moment[0],
        second_moment[0],
        grad_one,
        norm_one,
        (base_step + 1).astype(jnp.float32),
    )
    weight, moment_one, moment_two = adam_apply(
        weight, moment_one, moment_two, grad_two, norm_two, (base_step + 2).astype(jnp.float32)
    )
    return (weight, moment_one, moment_two)


def on_device(
    anchor, momentum, inner_weight, first_moment, second_moment, grad_first, grad_second, outer_step
):
    weight, moment_one, moment_two = inner_steps(
        inner_weight, first_moment, second_moment, grad_first, grad_second, outer_step
    )
    next_anchor, next_momentum = outer_update(anchor, momentum, inner_weight)
    next_inner = (next_anchor + (weight - inner_weight[0]))[None]
    return (next_anchor, next_momentum, next_inner, moment_one[None], moment_two[None])


def solution(mesh):
    split = Mesh(
        mesh.devices.reshape(mesh.shape["rep"], 8, 8, 4), ("rep", "fsdp_0", "fsdp_1", "fsdp_2")
    )
    return jax.shard_map(
        on_device,
        mesh=split,
        in_specs=(
            P(FSDP, None),
            P(FSDP, "rep"),
            P("rep", FSDP, None),
            P("rep", FSDP, None),
            P("rep", FSDP, None),
            P("rep", FSDP, None),
            P("rep", FSDP, None),
            P(),
        ),
        out_specs=(
            P(FSDP, None),
            P(FSDP, "rep"),
            P("rep", FSDP, None),
            P("rep", FSDP, None),
            P("rep", FSDP, None),
        ),
        check_vma=False,
    )
```

profile of v0, /device:TPU:1, one launch (start us, length us, event | category | flops | bytes accessed | tf_op | source)
XLA Modules:
  0.0 114.8 jit_solution(13627587275210715028)
XLA Ops:
  0.6 1.2 %bitcast_subtract_fusion.1 = f32[14,7168]{1,0:T(8,128)S(1)} fusion(f32[14,7168]{1,0:T(8,128)} %param.8, f32[1,14,7168]{2,0,1:T(1,128)} %param.10), kind=kLoop, calls=%fused_computation.26 | loop fusion | flops 100352 | bytes 1204224 | tf_op jit(solution)/shard_map/sub | solution.py:45
  1.9 0.2 reshape.41
  2.1 0.9 copy.25
  2.9 0.0 copy-start
  2.9 20.4 %all-to-all-start = ((f32[4,14,1792]{2,1,0:T(8,128)}), f32[4,14,1792]{2,1,0:T(8,128)S(1)}, u32[]{:S(2)}, u32[]{:S(2)}) async-start(f32[4,14,1792]{2,1,0:T(8,128)} %copy.25), calls=%async_computation | async-start | bytes 917504 | tf_op jit(solution)/shard_map/all_to_all | solution.py:22
  23.3 0.0 copy-start.3
  23.3 0.0 copy-done
  23.3 0.7 fusion.9
  24.0 0.2 copy-done.3
  24.2 1.4 %multiply_reduce_fusion = f32[]{:T(128)} fusion(bf16[1,14,7168]{2,1,0:T(8,128)(2,1)S(1)} %copy-done.3), kind=kLoop, calls=%fused_computation.35 | loop fusion | flops 301055 | bytes 200708 | tf_op jit(solution)/shard_map/reduce_sum | solution.py:61
  25.6 0.0 copy-start.4
  26.5 15.1 %all-reduce.1 = (f32[]{:T(128)}, f32[]{:T(128)}) all-reduce(f32[]{:T(128)} %multiply_reduce_fusion, f32[]{:T(128)} %fusion.9), channel_id=1, replica_groups=mesh['rep'=4,'fsdp_0'=8,'fsdp_1'=8,'fsdp_2'=4] {'fsdp_0'}, use_global_device_ids=true, to_apply=%region_6.0 | all-reduce | flops 2 | bytes 16 | tf_op jit(solution)/shard_map/psum | solution.py:27
  41.6 30.1 %all-reduce = (f32[]{:T(128)}, f32[]{:T(128)}) all-reduce(f32[]{:T(128)} %get-tuple-element.22, f32[]{:T(128)} %get-tuple-element.23), channel_id=1, replica_groups=mesh['rep'=4,'fsdp_0'=8,'fsdp_1'=8,'fsdp_2'=4] {'fsdp_1'}, use_global_device_ids=true, to_apply=%region_7.0 | all-reduce | flops 2 | bytes 16 | tf_op jit(solution)/shard_map/psum | solution.py:27
  71.7 9.1 %all-reduce.2 = (f32[]{:T(128)}, f32[]{:T(128)}) all-reduce(f32[]{:T(128)} %get-tuple-element.20, f32[]{:T(128)} %get-tuple-element.21), channel_id=1, replica_groups=mesh['rep'=4,'fsdp_0'=8,'fsdp_1'=8,'fsdp_2'=4] {'fsdp_2'}, use_global_device_ids=true, to_apply=%region_8.0 | all-reduce | flops 2 | bytes 16 | tf_op jit(solution)/shard_map/psum | solution.py:27
  82.3 0.0 copy-done.4
  82.3 0.0 copy-start.2
  82.3 2.3 %fusion.20 = (f32[1,14,7168]{2,0,1:T(1,128)}, f32[1,14,7168]{2,0,1:T(1,128)S(1)}, f32[1,14,7168]{2,0,1:T(1,128)S(1)}) fusion(f32[1,14,7168]{2,1,0:T(8,128)S(1)} %convert_multiply_fusion, f32[1,14,7168]{2,0,1:T(1,128)S(1)} %copy-done.4, bf16[1,14,7168]{2,1,0:T(8,128)(2,1)S(1)} %copy-done.3, f32[]{:T(128)S(6)} %min.7), kind=kLoop, calls=%fused_computation.33 | loop fusion | flops 1003520 | bytes 2207748 | tf_op jit(solution)/shard_map/add | solution.py:34
  84.6 0.0 copy-done.2
  84.6 0.2 fusion.8
  84.8 1.2 %copy.31 = f32[1,14,7168]{2,0,1:T(1,128)} copy(f32[1,14,7168]{2,1,0:T(8,128)S(1)} %fusion.8) | data formatting | bytes 802816
  86.0 0.0 copy-start.5
  86.0 0.0 all-to-all-done
  86.0 0.9 copy-done.5
  86.9 1.6 %multiply_subtract_fusion = (f32[14,1792]{1,0:T(8,128)S(1)}, f32[14,1792]{1,0:T(8,128)}) fusion(f32[14,7168]{1,0:T(8,128)} %param.8, s32[]{:T(128)S(6)} %select_n.3, f32[14,1792]{1,0:T(8,128)S(1)} %reduce_sum.27, f32[14,1792]{1,0:T(8,128)S(1)} %copy-done.5), kind=kLoop, calls=%fused_computation.38 | loop fusion | flops 175616 | bytes 501764 | tf_op jit(solution)/shard_map/sub | solution.py:50
  88.5 0.0 copy-start.1
  88.5 23.7 %all_gather.3 = f32[14,7168]{1,0:T(8,128)S(1)} all-gather(f32[14,1792]{1,0:T(8,128)S(1)} %get-tuple-element.26), channel_id=1, replica_groups=mesh['rep'=4,'fsdp_0'=8,'fsdp_1'=8,'fsdp_2'=4] {'rep'}, dimensions={1}, use_global_device_ids=true | all-gather | bytes 501760 | tf_op jit(solution)/shard_map/all_gather | solution.py:51
  112.1 0.0 copy-done.1
  112.1 0.8 fusion.7
  113.0 1.0 broadcast_in_dim.2
  114.0 0.8 copy.101
  (2 shorter events, 0.1 us)
Async XLA Ops:
  2.9 20.4 %copy-start = (bf16[1,14,7168]{2,1,0:T(8,128)(2,1)S(1)}, bf16[1,14,7168]{2,1,0:T(8,128)(2,1)}, u32[]{:S(2)}) copy-start(bf16[1,14,7168]{2,1,0:T(8,128)(2,1)} %param.13) | copy-start | bytes 602116
  2.9 83.1 %all-to-all-start = ((f32[4,14,1792]{2,1,0:T(8,128)}), f32[4,14,1792]{2,1,0:T(8,128)S(1)}, u32[]{:S(2)}, u32[]{:S(2)}) async-start(f32[4,14,1792]{2,1,0:T(8,128)} %copy.25), calls=%async_computation | async-start | bytes 917504 | tf_op jit(solution)/shard_map/all_to_all | solution.py:22
  23.3 0.9 copy-start.3
  25.6 56.7 %copy-start.4 = (f32[1,14,7168]{2,0,1:T(1,128)S(1)}, f32[1,14,7168]{2,0,1:T(1,128)}, u32[]{:S(2)}) copy-start(f32[1,14,7168]{2,0,1:T(1,128)} %param.12) | copy-start | bytes 1204228
  82.3 2.3 %copy-start.2 = (f32[1,14,7168]{2,0,1:T(1,128)S(1)}, f32[1,14,7168]{2,0,1:T(1,128)}, u32[]{:S(2)}) copy-start(f32[1,14,7168]{2,0,1:T(1,128)} %param.11) | copy-start | bytes 1204228
  86.0 0.9 copy-start.5
  88.5 23.7 %copy-start.1 = (f32[1,14,7168]{2,0,1:T(1,128)S(1)}, f32[1,14,7168]{2,0,1:T(1,128)}, u32[]{:S(2)}) copy-start(f32[1,14,7168]{2,0,1:T(1,128)} %param.10) | copy-start | bytes 1204228
where the time goes:
time: 115 us
  blocking collectives  77.9 us (68%)
  starting transfers between devices  20.4 us (18%)
  other arithmetic  8.32 us (7%)
  local copies, waits for them, and re-layouts  5.1 us (4%)
  between operations  3.02 us (3%)
    psum x3, blocking collectives, over_axes(): return functools.reduce(lax.psum, axes, x)  54.3 us
    all_gather x1, blocking collectives, outer_update(): next_anchor = lax.all_gather(anchor_share, 'rep', axis=1, tiled=True)  23.7 us
    all_to_all x1, starting transfers between devices, summed_on_arrival(): lax.all_to_all(pieces, axis, split_axis=0, concat_axis=0, tiled=True)  20.4 us
    unnamed x14, local copies, waits for them, and re-layouts  3.03 us
  transfers between devices with their start and end apart: 1, of which 0 were waited for; matrix products, arithmetic and copies ran while one was open for 5% of the time, Pallas kernels for 0%

commit v1 on v0

v1 whole, which is shorter than its diff:
```python
import math

import jax
import jax.numpy as jnp
from jax import lax
from jax.sharding import Mesh
from jax.sharding import PartitionSpec as P

D = 3584
FF = 7168
REP = ("z_hi", "core")
FSDP = ("fsdp_0", "fsdp_1", "fsdp_2")


def all_summed(values, axes):
    count = 1
    for axis in axes:
        count *= lax.axis_size(axis)
    spread = jnp.broadcast_to(values[None], (count,) + values.shape)
    return lax.all_to_all(spread, axes, 0, 0, tiled=False).sum(axis=0)


def adam_apply(weight, first_moment, second_moment, grad_full, square_sum, step_count):
    factor = jnp.minimum(1.0, 0.5 * math.sqrt(D * FF) / (jnp.sqrt(square_sum) + 1e-06))
    scaled = factor * grad_full
    first_moment = 0.9 * first_moment + 0.1 * scaled
    second_moment = 0.95 * second_moment + 0.05 * scaled * scaled
    first_hat = first_moment / (1.0 - jnp.power(jnp.float32(0.9), step_count))
    second_hat = second_moment / (1.0 - jnp.power(jnp.float32(0.95), step_count))
    weight = weight - 0.1 * (first_hat / (jnp.sqrt(second_hat) + 1e-08) + 0.1 * weight)
    return (weight, first_moment, second_moment)


def outer_update(anchor, momentum, inner_weight):
    replicas = lax.axis_size("z_hi") * lax.axis_size("core")
    rows, cols = anchor.shape
    block = cols // replicas
    hi = lax.axis_index("z_hi")
    pseudo = (anchor - inner_weight[0]).reshape(rows, 2, 2, block)
    on_chip = lax.all_to_all(pseudo, "core", 2, 2, tiled=True).sum(axis=2)
    payload = jnp.concatenate([on_chip, momentum[:, None, :]], axis=1)
    both = lax.all_gather(payload, "z_hi", axis=0, tiled=False)
    delta_half = both[0, :, :2] + both[1, :, :2]
    outer_grad = delta_half / replicas
    momentum_half = jnp.stack([both[0, :, 2], both[1, :, 2]], axis=1)
    next_momentum = 0.9 * momentum_half + outer_grad
    lo = lax.axis_index("core")
    anchor_half = lax.dynamic_index_in_dim(anchor.reshape(rows, 2, 2, block), lo, 2, keepdims=False)
    anchor_half = anchor_half - 0.7 * (outer_grad + 0.9 * next_momentum)
    next_anchor = lax.all_gather(anchor_half, "core", axis=2, tiled=False).reshape(rows, cols)
    own_momentum = lax.dynamic_index_in_dim(next_momentum, hi, 1, keepdims=False)
    return (next_anchor, own_momentum)


def inner_steps(inner_weight, first_moment, second_moment, grad_first, grad_second, outer_step):
    base_step = 2 * outer_step[0]
    grad_one = grad_first[0].astype(jnp.float32)
    grad_two = grad_second[0].astype(jnp.float32)
    squares = jnp.stack([jnp.sum(grad_one * grad_one), jnp.sum(grad_two * grad_two)])
    norm_one, norm_two = all_summed(squares, FSDP)
    weight, moment_one, moment_two = adam_apply(
        inner_weight[0],
        first_moment[0],
        second_moment[0],
        grad_one,
        norm_one,
        (base_step + 1).astype(jnp.float32),
    )
    weight, moment_one, moment_two = adam_apply(
        weight, moment_one, moment_two, grad_two, norm_two, (base_step + 2).astype(jnp.float32)
    )
    return (weight, moment_one, moment_two)


def on_device(
    anchor, momentum, inner_weight, first_moment, second_moment, grad_first, grad_second, outer_step
):
    weight, moment_one, moment_two = inner_steps(
        inner_weight, first_moment, second_moment, grad_first, grad_second, outer_step
    )
    next_anchor, next_momentum = outer_update(anchor, momentum, inner_weight)
    next_inner = (next_anchor + (weight - inner_weight[0]))[None]
    return (next_anchor, next_momentum, next_inner, moment_one[None], moment_two[None])


def solution(mesh):
    fsdp = mesh.shape["fsdp"]
    split = Mesh(
        mesh.devices.reshape(2, mesh.shape["rep"] // 2, fsdp // 32, 8, 4),
        REP + FSDP,
    )
    return jax.shard_map(
        on_device,
        mesh=split,
        in_specs=(
            P(FSDP, None),
            P(FSDP, REP),
            P(REP, FSDP, None),
            P(REP, FSDP, None),
            P(REP, FSDP, None),
            P(REP, FSDP, None),
            P(REP, FSDP, None),
            P(),
        ),
        out_specs=(
            P(FSDP, None),
            P(FSDP, REP),
            P(REP, FSDP, None),
            P(REP, FSDP, None),
            P(REP, FSDP, None),
        ),
        check_vma=False,
    )
```

time: 115 us -> 96.7 us (0.84)
  the two profiles are of different devices: /device:TPU:1 before, /device:TPU:255 now
where the time goes in v1:
time: 96.7 us; the launch traced here: 96.3 us
  blocking collectives  47.9 us (50%)
  starting transfers between devices  28.4 us (29%)
  local copies, waits for them, and re-layouts  10.2 us (11%)
  other arithmetic  6.67 us (7%)
  between operations  3.05 us (3%)
    all_gather x1, blocking collectives, outer_update(): both = lax.all_gather(payload, 'z_hi', axis=0, tiled=False)  45.1 us
    all_to_all x1, starting transfers between devices, all_summed(): return lax.all_to_all(spread, axes, 0, 0, tiled=False).sum(axis=0)  24.2 us
    unnamed x18, local copies, waits for them, and re-layouts  5.16 us
    all_to_all x1, starting transfers between devices, outer_update(): on_chip = lax.all_to_all(pseudo, 'core', 2, 2, tiled=True).sum(axis=2)  4.26 us
    all_gather x1, blocking collectives, outer_update(): lax.all_gather(anchor_half, 'core', axis=2, tiled=False).reshape(rows, cols)  2.79 us
  transfers between devices with their start and end apart: 2, of which 0 were waited for; matrix products, arithmetic and copies ran while one was open for 8% of the time, Pallas kernels for 0%

profile of v1, /device:TPU:255, one launch (start us, length us, event | category | flops | bytes accessed | tf_op | source)
XLA Modules:
  0.0 96.3 jit_solution(3631154148242734315)
XLA Ops:
  0.6 1.2 %fusion.2 = f32[14,7168]{1,0:T(8,128)S(1)} fusion(f32[14,7168]{1,0:T(8,128)} %param.8, f32[1,14,7168]{2,0,1:T(1,128)} %param.10), kind=kLoop, calls=%fused_computation.12 | loop fusion | flops 100352 | bytes 1204224 | tf_op jit(solution)/shard_map/sub | solution.py:39
  1.9 0.3 reshape.132
  2.2 1.0 copy.69
  3.2 4.3 %all-to-all-start = ((f32[14,2,2,1792]{3,1,0,2:T(2,128)}), f32[14,2,2,1792]{3,1,0,2:T(2,128)S(1)}, u32[]{:S(2)}, u32[]{:S(2)}) async-start(f32[14,2,2,1792]{3,1,0,2:T(2,128)} %copy.69), calls=%async_computation | async-start | bytes 802816 | tf_op jit(solution)/shard_map/all_to_all | solution.py:40
  7.4 0.3 reshape.131
  7.8 0.6 copy-done.2
  8.4 0.7 fusion.9
  9.1 0.2 copy-done.3
  9.3 0.7 fusion.8
  10.0 0.2 copy-done.6
  10.3 1.4 %pad_maximum_fusion.1 = f32[2]{0:T(128)S(1)} fusion(f32[1]{0:T(128)} %bitcast.9, f32[1]{0:T(128)} %bitcast.8), kind=kLoop, calls=%fused_computation.43 | loop fusion | flops 2 | bytes 16 | tf_op jit(solution)/shard_map/stack | solution.py:59
  11.7 0.7 broadcast_in_dim.5
  12.4 24.2 %all-to-all-start.1 = ((f32[256,1,2]{2,1,0:T(1,128)}), f32[256,1,2]{2,1,0:T(1,128)S(1)}, u32[]{:S(2)}, u32[]{:S(2)}) async-start(f32[256,1,2]{2,1,0:T(1,128)} %broadcast_in_dim.5), calls=%async_computation.1 | async-start | bytes 262144 | tf_op jit(solution)/shard_map/all_to_all | solution.py:20
  36.6 0.3 reduce_sum.36
  36.9 0.2 pad_maximum_fusion
  37.1 45.1 %all-gather = f32[28,3,1792]{2,1,0:T(4,128)S(1)} all-gather(f32[14,3,1792]{2,1,0:T(4,128)S(1)} %pad_maximum_fusion), channel_id=2, replica_groups=mesh['z_hi'=2,'core'=2,'fsdp_0'=8,'fsdp_1'=8,'fsdp_2'=4] {'z_hi'}, dimensions={0}, use_global_device_ids=true | all-gather | bytes 903168 | tf_op jit(solution)/shard_map/all_gather | solution.py:42
  82.2 0.1 fusion.18
  82.3 0.3 slice_bitcast_fusion.2
  82.6 0.2 constant_dynamic-slice_fusion
  82.8 0.4 fusion.16
  83.2 0.4 dynamic-slice_add_fusion
  83.7 2.8 %all_gather.12 = f32[14,2,2,1792]{3,1,0,2:T(2,128)S(1)} all-gather(f32[14,2,1,1792]{3,1,0,2:T(2,128)S(1)} %fusion.16), channel_id=1, replica_groups=mesh['z_hi'=2,'core'=2,'fsdp_0'=8,'fsdp_1'=8,'fsdp_2'=4] {'core'}, dimensions={2}, use_global_device_ids=true | all-gather | bytes 602112 | tf_op jit(solution)/shard_map/all_gather | solution.py:50
  87.3 0.2 copy.71
  87.5 0.3 reshape.134
  87.9 1.1 %reshape.133 = f32[14,7168]{1,0:T(8,128)} reshape(f32[14,2,2,1792]{3,2,1,0:T(2,128)S(1)} %copy.71) | data formatting | bytes 802816 | tf_op jit(solution)/shard_map/reshape | solution.py:50
  88.9 0.7 copy.126
  89.6 0.3 reduce_sum.39
  89.9 0.6 fusion.19
  92.0 0.8 fusion.11
  92.8 1.2 %copy.81 = f32[1,14,7168]{2,0,1:T(1,128)} copy(f32[1,14,7168]{2,1,0:T(8,128)S(1)} %get-tuple-element.25) | data formatting | bytes 802816
  94.0 1.2 %copy.79 = f32[1,14,7168]{2,0,1:T(1,128)} copy(f32[1,14,7168]{2,1,0:T(8,128)S(1)} %get-tuple-element.26) | data formatting | bytes 802816
  95.1 1.2 %copy.80 = f32[1,14,7168]{2,0,1:T(1,128)} copy(f32[1,14,7168]{2,1,0:T(8,128)S(1)} %get-tuple-element.27) | data formatting | bytes 802816
  (14 shorter events, 0.1 us)
Async XLA Ops:
  3.2 4.3 %copy-start = (f32[14,7168]{1,0:T(8,128)S(1)}, f32[14,7168]{1,0:T(8,128)}, u32[]{:S(2)}) copy-start(f32[14,7168]{1,0:T(8,128)} %param.8) | copy-start | bytes 1204228
  3.2 8.5 %all-to-all-start = ((f32[14,2,2,1792]{3,1,0,2:T(2,128)}), f32[14,2,2,1792]{3,1,0,2:T(2,128)S(1)}, u32[]{:S(2)}, u32[]{:S(2)}) async-start(f32[14,2,2,1792]{3,1,0,2:T(2,128)} %copy.69), calls=%async_computation | async-start | bytes 802816 | tf_op jit(solution)/shard_map/all_to_all | solution.py:40
  7.4 0.9 copy-start.2
  8.4 0.9 copy-start.3
  9.3 0.9 copy-start.6
  12.4 77.2 %all-to-all-start.1 = ((f32[256,1,2]{2,1,0:T(1,128)}), f32[256,1,2]{2,1,0:T(1,128)S(1)}, u32[]{:S(2)}, u32[]{:S(2)}) async-start(f32[256,1,2]{2,1,0:T(1,128)} %broadcast_in_dim.5), calls=%async_computation.1 | async-start | bytes 262144 | tf_op jit(solution)/shard_map/all_to_all | solution.py:20
  87.8 4.1 %copy-start.1 = (f32[1,14,7168]{2,0,1:T(1,128)S(1)}, f32[1,14,7168]{2,0,1:T(1,128)}, u32[]{:S(2)}) copy-start(f32[1,14,7168]{2,0,1:T(1,128)} %param.10) | copy-start | bytes 1204228
  87.8 4.1 %copy-start.4 = (f32[1,14,7168]{2,0,1:T(1,128)S(1)}, f32[1,14,7168]{2,0,1:T(1,128)}, u32[]{:S(2)}) copy-start(f32[1,14,7168]{2,0,1:T(1,128)} %param.12) | copy-start | bytes 1204228
  87.8 4.1 %copy-start.5 = (f32[1,14,7168]{2,0,1:T(1,128)S(1)}, f32[1,14,7168]{2,0,1:T(1,128)}, u32[]{:S(2)}) copy-start(f32[1,14,7168]{2,0,1:T(1,128)} %param.11) | copy-start | bytes 1204228

commit v2 on v1

--- a/solution.py
+++ b/solution.py
@@ -36,20 +36,24 @@
     rows, cols = anchor.shape
     block = cols // replicas
     hi = lax.axis_index("z_hi")
+    lo = lax.axis_index("core")
     pseudo = (anchor - inner_weight[0]).reshape(rows, 2, 2, block)
     on_chip = lax.all_to_all(pseudo, "core", 2, 2, tiled=True).sum(axis=2)
-    payload = jnp.concatenate([on_chip, momentum[:, None, :]], axis=1)
+    anchor_half = lax.dynamic_index_in_dim(anchor.reshape(rows, 2, 2, block), lo, 2, keepdims=False)
+    own_sum = lax.dynamic_index_in_dim(on_chip, hi, 1, keepdims=False)
+    other_sum = lax.dynamic_index_in_dim(on_chip, 1 - hi, 1, keepdims=False)
+    own_anchor = lax.dynamic_index_in_dim(anchor_half, hi, 1, keepdims=False)
+    folded = own_anchor - 0.567 * momentum - 0.3325 * own_sum
+    payload = jnp.stack([folded, other_sum], axis=1)
     both = lax.all_gather(payload, "z_hi", axis=0, tiled=False)
-    delta_half = both[0, :, :2] + both[1, :, :2]
-    outer_grad = delta_half / replicas
-    momentum_half = jnp.stack([both[0, :, 2], both[1, :, 2]], axis=1)
-    next_momentum = 0.9 * momentum_half + outer_grad
-    lo = lax.axis_index("core")
-    anchor_half = lax.dynamic_index_in_dim(anchor.reshape(rows, 2, 2, block), lo, 2, keepdims=False)
-    anchor_half = anchor_half - 0.7 * (outer_grad + 0.9 * next_momentum)
+    anchor_half = jnp.stack(
+        [both[0, :, 0] - 0.3325 * both[1, :, 1], both[1, :, 0] - 0.3325 * both[0, :, 1]], axis=1
+    )
     next_anchor = lax.all_gather(anchor_half, "core", axis=2, tiled=False).reshape(rows, cols)
-    own_momentum = lax.dynamic_index_in_dim(next_momentum, hi, 1, keepdims=False)
-    return (next_anchor, own_momentum)
+    arrived = lax.dynamic_index_in_dim(both, 1 - hi, 0, keepdims=False)[:, 1]
+    outer_grad = (own_sum + arrived) / replicas
+    next_momentum = 0.9 * momentum + outer_grad
+    return (next_anchor, next_momentum)
 
 
 def inner_steps(inner_weight, first_moment, second_moment, grad_first, grad_second, outer_step):

time: 96.7 us -> 82.6 us (0.85)
  the two profiles are of different devices: /device:TPU:255 before, /device:TPU:249 now
where the time goes in v2:
time: 82.6 us; the launch traced here: 82.2 us
  blocking collectives  34.1 us (41%)
  starting transfers between devices  28.5 us (35%)
  local copies, waits for them, and re-layouts  9.64 us (12%)
  other arithmetic  6.86 us (8%)
  between operations  3.1 us (4%)
    all_gather x1, blocking collectives, outer_update(): both = lax.all_gather(payload, 'z_hi', axis=0, tiled=False)  31.7 us
    all_to_all x1, starting transfers between devices, all_summed(): return lax.all_to_all(spread, axes, 0, 0, tiled=False).sum(axis=0)  24.2 us
    unnamed x19, local copies, waits for them, and re-layouts  5.89 us
    all_to_all x1, starting transfers between devices, outer_update(): on_chip = lax.all_to_all(pseudo, 'core', 2, 2, tiled=True).sum(axis=2)  4.26 us
    all_gather x1, blocking collectives, outer_update(): lax.all_gather(anchor_half, 'core', axis=2, tiled=False).reshape(rows, cols)  2.38 us
  transfers between devices with their start and end apart: 2, of which 0 were waited for; matrix products, arithmetic and copies ran while one was open for 8% of the time, Pallas kernels for 0%

profile of v2, /device:TPU:249, one launch (start us, length us, event | category | flops | bytes accessed | tf_op | source)
XLA Modules:
  0.0 82.2 jit_solution(6786950026732543954)
XLA Ops:
  0.6 1.2 %fusion.2 = f32[14,7168]{1,0:T(8,128)S(1)} fusion(f32[14,7168]{1,0:T(8,128)} %param.8, f32[1,14,7168]{2,0,1:T(1,128)} %param.10), kind=kLoop, calls=%fused_computation.12 | loop fusion | flops 100352 | bytes 1204224 | tf_op jit(solution)/shard_map/sub | solution.py:40
  1.9 0.3 reshape.116
  2.2 1.0 %copy.76 = f32[14,2,2,1792]{3,1,0,2:T(2,128)} copy(f32[14,2,2,1792]{3,2,1,0:T(2,128)S(1)} %reshape.116) | data formatting | bytes 802816 | tf_op jit(solution)/shard_map/reshape | solution.py:40
  3.2 4.3 %all-to-all-start = ((f32[14,2,2,1792]{3,1,0,2:T(2,128)}), f32[14,2,2,1792]{3,1,0,2:T(2,128)S(1)}, u32[]{:S(2)}, u32[]{:S(2)}) async-start(f32[14,2,2,1792]{3,1,0,2:T(2,128)} %copy.76), calls=%async_computation | async-start | bytes 802816 | tf_op jit(solution)/shard_map/all_to_all | solution.py:41
  7.4 0.3 reshape.115
  7.8 0.6 copy-done.2
  8.4 0.7 fusion.9
  9.1 0.7 fusion.8
  9.8 1.4 %pad_maximum_fusion.2 = f32[2]{0:T(128)S(1)} fusion(f32[1]{0:T(128)} %bitcast.8, f32[1]{0:T(128)} %bitcast.7), kind=kLoop, calls=%fused_computation.45 | loop fusion | flops 2 | bytes 16 | tf_op jit(solution)/shard_map/stack | solution.py:63
  11.2 0.7 broadcast_in_dim.2
  11.9 24.2 %all-to-all-start.1 = ((f32[256,1,2]{2,1,0:T(1,128)}), f32[256,1,2]{2,1,0:T(1,128)S(1)}, u32[]{:S(2)}, u32[]{:S(2)}) async-start(f32[256,1,2]{2,1,0:T(1,128)} %broadcast_in_dim.2), calls=%async_computation.1 | async-start | bytes 262144 | tf_op jit(solution)/shard_map/all_to_all | solution.py:20
  36.2 0.3 reduce_sum.36
  36.5 0.2 constant_dynamic-slice_fusion.1
  36.7 0.1 constant_dynamic-slice_fusion.2
  36.8 0.8 copy-done.4
  37.6 0.1 stack.21
  37.7 0.2 pad_maximum_fusion
  37.9 31.7 %all-gather = f32[28,2,1792]{2,1,0:T(2,128)S(1)} all-gather(f32[14,2,1792]{2,1,0:T(2,128)S(1)} %pad_maximum_fusion), channel_id=2, replica_groups=mesh['z_hi'=2,'core'=2,'fsdp_0'=8,'fsdp_1'=8,'fsdp_2'=4] {'z_hi'}, dimensions={0}, use_global_device_ids=true | all-gather | bytes 602112 | tf_op jit(solution)/shard_map/all_gather | solution.py:48
  69.6 0.3 fusion.20
  69.9 0.1 slice.24
  70.0 0.7 fusion.16
  70.7 0.2 pad_maximum_fusion.1
  70.9 2.4 %all-gather.1 = f32[14,2,3584]{2,1,0:T(2,128)S(1)} all-gather(f32[14,2,1792]{2,1,0:T(2,128)S(1)} %pad_maximum_fusion.1), channel_id=3, replica_groups=mesh['z_hi'=2,'core'=2,'fsdp_0'=8,'fsdp_1'=8,'fsdp_2'=4] {'core'}, dimensions={2}, use_global_device_ids=true | all-gather | bytes 602112 | tf_op jit(solution)/shard_map/all_gather | solution.py:52
  74.1 0.2 pad.6
  74.3 0.3 reshape.118
  74.6 0.9 %copy.97 = f32[2,8,2,3584]{3,1,2,0:T(8,128)} copy(f32[2,8,2,3584]{3,2,1,0:T(2,128)S(1)} %bitcast.38) | data formatting | bytes 917504
  75.5 0.3 reduce_sum.39
  75.8 0.6 fusion.22
  77.9 0.8 %fusion.11 = (f32[1,14,7168]{2,1,0:T(8,128)S(1)}, f32[1,14,7168]{2,1,0:T(8,128)S(1)}, f32[1,14,7168]{2,1,0:T(8,128)S(1)}) fusion(bf16[1,14,7168]{2,1,0:T(8,128)(2,1)S(1)} %copy-done.2, f32[]{:T(128)} %bitcast.12, bf16[1,14,7168]{2,1,0:T(8,128)(2,1)S(1)} %copy-done.3, f32[1,14,7168]{2,0,1:T(1,128)S(1)} %copy-done.5, f32[]{:T(128)} %bitcast.9, ...), kind=kLoop, calls=%fused_computation.21 | loop fusion | flops 3612672 | bytes 3211288 | tf_op jit(solution)/shard_map/add | solution.py:27
  78.7 1.2 %copy.88 = f32[1,14,7168]{2,0,1:T(1,128)} copy(f32[1,14,7168]{2,1,0:T(8,128)S(1)} %get-tuple-element.30) | data formatting | bytes 802816
  79.9 1.2 %copy.86 = f32[1,14,7168]{2,0,1:T(1,128)} copy(f32[1,14,7168]{2,1,0:T(8,128)S(1)} %get-tuple-element.31) | data formatting | bytes 802816
  81.0 1.2 %copy.87 = f32[1,14,7168]{2,0,1:T(1,128)} copy(f32[1,14,7168]{2,1,0:T(8,128)S(1)} %get-tuple-element.32) | data formatting | bytes 802816
  (16 shorter events, 0.1 us)
Async XLA Ops:
  3.2 4.3 %copy-start = (f32[14,7168]{1,0:T(8,128)S(1)}, f32[14,7168]{1,0:T(8,128)}, u32[]{:S(2)}) copy-start(f32[14,7168]{1,0:T(8,128)} %param.8) | copy-start | bytes 1204228
  3.2 8.0 %all-to-all-start = ((f32[14,2,2,1792]{3,1,0,2:T(2,128)}), f32[14,2,2,1792]{3,1,0,2:T(2,128)S(1)}, u32[]{:S(2)}, u32[]{:S(2)}) async-start(f32[14,2,2,1792]{3,1,0,2:T(2,128)} %copy.76), calls=%async_computation | async-start | bytes 802816 | tf_op jit(solution)/shard_map/all_to_all | solution.py:41
  7.4 0.9 %copy-start.2 = (bf16[1,14,7168]{2,1,0:T(8,128)(2,1)S(1)}, bf16[1,14,7168]{2,1,0:T(8,128)(2,1)}, u32[]{:S(2)}) copy-start(bf16[1,14,7168]{2,1,0:T(8,128)(2,1)} %param.14) | copy-start | bytes 602116
  7.8 1.3 %copy-start.3 = (bf16[1,14,7168]{2,1,0:T(8,128)(2,1)S(1)}, bf16[1,14,7168]{2,1,0:T(8,128)(2,1)}, u32[]{:S(2)}) copy-start(bf16[1,14,7168]{2,1,0:T(8,128)(2,1)} %param.13) | copy-start | bytes 602116
  11.9 63.6 %all-to-all-start.1 = ((f32[256,1,2]{2,1,0:T(1,128)}), f32[256,1,2]{2,1,0:T(1,128)S(1)}, u32[]{:S(2)}, u32[]{:S(2)}) async-start(f32[256,1,2]{2,1,0:T(1,128)} %broadcast_in_dim.2), calls=%async_computation.1 | async-start | bytes 262144 | tf_op jit(solution)/shard_map/all_to_all | solution.py:20
  36.7 0.9 %copy-start.4 = (f32[14,1792]{1,0:T(8,128)S(1)}, f32[14,1792]{1,0:T(8,128)}, u32[]{:S(2)}) copy-start(f32[14,1792]{1,0:T(8,128)} %param.9) | copy-start | bytes 301060
  74.3 3.6 %copy-start.6 = (f32[1,14,7168]{2,0,1:T(1,128)S(1)}, f32[1,14,7168]{2,0,1:T(1,128)}, u32[]{:S(2)}) copy-start(f32[1,14,7168]{2,0,1:T(1,128)} %param.11) | copy-start | bytes 1204228
  74.6 3.2 %copy-start.1 = (f32[1,14,7168]{2,0,1:T(1,128)S(1)}, f32[1,14,7168]{2,0,1:T(1,128)}, u32[]{:S(2)}) copy-start(f32[1,14,7168]{2,0,1:T(1,128)} %param.10) | copy-start | bytes 1204228
  74.6 3.2 %copy-start.5 = (f32[1,14,7168]{2,0,1:T(1,128)S(1)}, f32[1,14,7168]{2,0,1:T(1,128)}, u32[]{:S(2)}) copy-start(f32[1,14,7168]{2,0,1:T(1,128)} %param.12) | copy-start | bytes 1204228

commit v3 on v2

--- a/solution.py
+++ b/solution.py
@@ -45,13 +45,12 @@
     own_anchor = lax.dynamic_index_in_dim(anchor_half, hi, 1, keepdims=False)
     folded = own_anchor - 0.567 * momentum - 0.3325 * own_sum
     payload = jnp.stack([folded, other_sum], axis=1)
-    both = lax.all_gather(payload, "z_hi", axis=0, tiled=False)
-    anchor_half = jnp.stack(
-        [both[0, :, 0] - 0.3325 * both[1, :, 1], both[1, :, 0] - 0.3325 * both[0, :, 1]], axis=1
-    )
+    arrived = lax.ppermute(payload, "z_hi", [(0, 1), (1, 0)])
+    mine = folded - 0.3325 * arrived[:, 1]
+    theirs = arrived[:, 0] - 0.3325 * other_sum
+    anchor_half = jnp.where(hi == 0, jnp.stack([mine, theirs], axis=1), jnp.stack([theirs, mine], axis=1))
     next_anchor = lax.all_gather(anchor_half, "core", axis=2, tiled=False).reshape(rows, cols)
-    arrived = lax.dynamic_index_in_dim(both, 1 - hi, 0, keepdims=False)[:, 1]
-    outer_grad = (own_sum + arrived) / replicas
+    outer_grad = (own_sum + arrived[:, 1]) / replicas
     next_momentum = 0.9 * momentum + outer_grad
     return (next_anchor, next_momentum)
 

time: 82.6 us -> 83.8 us (1.015)
  the two profiles are of different devices: /device:TPU:249 before, /device:TPU:1 now
where the time goes in v3:
time: 83.8 us; the launch traced here: 83.4 us
  starting transfers between devices  44.6 us (53%)
  waiting for transfers between devices  15 us (18%)
  local copies, waits for them, and re-layouts  9.26 us (11%)
  other arithmetic  6.7 us (8%)
  blocking collectives  4.76 us (6%)
  between operations  3.11 us (4%)
    all_to_all x1, starting transfers between devices, all_summed(): return lax.all_to_all(spread, axes, 0, 0, tiled=False).sum(axis=0)  20.3 us
    all_to_all x1, starting transfers between devices, outer_update(): on_chip = lax.all_to_all(pseudo, 'core', 2, 2, tiled=True).sum(axis=2)  17.7 us
    all_to_all x1, waiting for transfers between devices, all_summed(): return lax.all_to_all(spread, axes, 0, 0, tiled=False).sum(axis=0)  14.1 us
    ppermute x1, starting transfers between devices, outer_update(): arrived = lax.ppermute(payload, 'z_hi', [(0, 1), (1, 0)])  6.56 us
    all_gather x1, blocking collectives, outer_update(): lax.all_gather(anchor_half, 'core', axis=2, tiled=False).reshape(rows, cols)  4.76 us
    unnamed x17, local copies, waits for them, and re-layouts  4.34 us
  transfers between devices with their start and end apart: 3, of which 2 were waited for; matrix products, arithmetic and copies ran while one was open for 6% of the time, Pallas kernels for 0%

profile of v3, /device:TPU:1, one launch (start us, length us, event | category | flops | bytes accessed | tf_op | source)
XLA Modules:
  0.0 83.4 jit_solution(5774181794038229754)
XLA Ops:
  0.6 1.2 %fusion.2 = f32[14,7168]{1,0:T(8,128)S(1)} fusion(f32[14,7168]{1,0:T(8,128)} %param.8, f32[1,14,7168]{2,0,1:T(1,128)} %param.10), kind=kLoop, calls=%fused_computation.12 | loop fusion | flops 100352 | bytes 1204224 | tf_op jit(solution)/shard_map/sub | solution.py:40
  1.9 0.3 reshape.129
  2.2 1.0 %copy.66 = f32[14,2,2,1792]{3,1,0,2:T(2,128)} copy(f32[14,2,2,1792]{3,2,1,0:T(2,128)S(1)} %reshape.129) | data formatting | bytes 802816 | tf_op jit(solution)/shard_map/reshape | solution.py:40
  3.2 17.7 %all-to-all-start = ((f32[14,2,2,1792]{3,1,0,2:T(2,128)}), f32[14,2,2,1792]{3,1,0,2:T(2,128)S(1)}, u32[]{:S(2)}, u32[]{:S(2)}) async-start(f32[14,2,2,1792]{3,1,0,2:T(2,128)} %copy.66), calls=%async_computation | async-start | bytes 802816 | tf_op jit(solution)/shard_map/all_to_all | solution.py:41
  20.9 0.3 reshape.128
  21.3 0.9 %all-to-all-done = f32[14,2,2,1792]{3,1,0,2:T(2,128)S(1)} async-done(((f32[14,2,2,1792]{3,1,0,2:T(2,128)}), f32[14,2,2,1792]{3,1,0,2:T(2,128)S(1)}, u32[]{:S(2)}, u32[]{:S(2)}) %all-to-all-start) | async-done | bytes 401440 | tf_op jit(solution)/shard_map/all_to_all | solution.py:41
  22.2 0.3 reduce_sum.36
  22.5 0.2 constant_dynamic-slice_fusion.1
  22.7 0.1 constant_dynamic-slice_fusion.2
  22.9 0.8 copy-done.4
  23.7 6.6 %collective-permute-start = (f32[14,2,1792]{2,0,1:T(8,128)S(1)}, f32[14,2,1792]{2,0,1:T(8,128)S(1)}, u32[]{:S(2)}, u32[]{:S(2)}) collective-permute-start(f32[14,2,1792]{2,0,1:T(8,128)S(1)} %pad_maximum_fusion), channel_id=1, source_target_pairs={{0,512},{512,0},{1,513},{513,1},{2,514},{514,2},{3,515},{515,3},{4... | collective-permute-start | bytes 602120 | tf_op jit(solution)/shard_map/ppermute | solution.py:48
  30.3 0.7 fusion.8
  31.0 0.7 fusion.9
  31.7 1.4 %pad_maximum_fusion.1 = f32[2]{0:T(128)S(1)} fusion(f32[1]{0:T(128)} %bitcast.7, f32[1]{0:T(128)} %bitcast.6), kind=kLoop, calls=%fused_computation.41 | loop fusion | flops 2 | bytes 16 | tf_op jit(solution)/shard_map/stack | solution.py:62
  33.1 0.7 broadcast_in_dim.2
  33.8 20.3 %all-to-all-start.1 = ((f32[256,1,2]{2,1,0:T(1,128)}), f32[256,1,2]{2,1,0:T(1,128)S(1)}, u32[]{:S(2)}, u32[]{:S(2)}) async-start(f32[256,1,2]{2,1,0:T(1,128)} %broadcast_in_dim.2), calls=%async_computation.1 | async-start | bytes 262144 | tf_op jit(solution)/shard_map/all_to_all | solution.py:20
  54.9 14.1 %all-to-all-done.1 = f32[256,1,2]{2,1,0:T(1,128)S(1)} async-done(((f32[256,1,2]{2,1,0:T(1,128)}), f32[256,1,2]{2,1,0:T(1,128)S(1)}, u32[]{:S(2)}, u32[]{:S(2)}) %all-to-all-start.1) | async-done | bytes 2080 | tf_op jit(solution)/shard_map/all_to_all | solution.py:20
  69.0 0.3 reduce_sum.39
  69.3 0.6 fusion.20
  71.3 0.7 fusion.16
  72.0 0.1 stack.32
  72.1 0.2 fusion.18
  72.3 0.3 maximum_select_fusion
  72.6 4.8 %all_gather.4 = f32[14,2,2,1792]{3,1,2,0:T(2,128)S(1)} all-gather(f32[14,2,1,1792]{3,1,2,0:T(2,128)S(1)} %maximum_select_fusion), channel_id=1, replica_groups=mesh['z_hi'=2,'core'=2,'fsdp_0'=8,'fsdp_1'=8,'fsdp_2'=4] {'core'}, dimensions={2}, use_global_device_ids=true | all-gather | bytes 602112 | tf_op jit(solution)/shard_map/all_gather | solution.py:52
  77.4 0.2 copy.72
  77.6 0.3 reshape.131
  77.9 1.1 %reshape.130 = f32[14,7168]{1,0:T(8,128)} reshape(f32[14,2,2,1792]{3,2,1,0:T(2,128)S(1)} %copy.72) | data formatting | bytes 802816 | tf_op jit(solution)/shard_map/reshape | solution.py:52
  79.0 0.0 copy-done.5
  79.1 0.8 fusion.11
  79.9 1.2 %copy.80 = f32[1,14,7168]{2,0,1:T(1,128)} copy(f32[1,14,7168]{2,1,0:T(8,128)S(1)} %get-tuple-element.21) | data formatting | bytes 802816
  81.1 1.2 %copy.81 = f32[1,14,7168]{2,0,1:T(1,128)} copy(f32[1,14,7168]{2,1,0:T(8,128)S(1)} %get-tuple-element.22) | data formatting | bytes 802816
  82.2 1.2 %copy.82 = f32[1,14,7168]{2,0,1:T(1,128)} copy(f32[1,14,7168]{2,1,0:T(8,128)S(1)} %get-tuple-element.20) | data formatting | bytes 802816
  (17 shorter events, 0.1 us)
Async XLA Ops:
  3.2 17.7 %copy-start = (f32[14,7168]{1,0:T(8,128)S(1)}, f32[14,7168]{1,0:T(8,128)}, u32[]{:S(2)}) copy-start(f32[14,7168]{1,0:T(8,128)} %param.8) | copy-start | bytes 1204228
  3.2 19.0 %all-to-all-start = ((f32[14,2,2,1792]{3,1,0,2:T(2,128)}), f32[14,2,2,1792]{3,1,0,2:T(2,128)S(1)}, u32[]{:S(2)}, u32[]{:S(2)}) async-start(f32[14,2,2,1792]{3,1,0,2:T(2,128)} %copy.66), calls=%async_computation | async-start | bytes 802816 | tf_op jit(solution)/shard_map/all_to_all | solution.py:41
  22.7 0.9 %copy-start.4 = (f32[14,1792]{1,0:T(8,128)S(1)}, f32[14,1792]{1,0:T(8,128)}, u32[]{:S(2)}) copy-start(f32[14,1792]{1,0:T(8,128)} %param.9) | copy-start | bytes 301060
  23.7 6.6 %copy-start.3 = (bf16[1,14,7168]{2,1,0:T(8,128)(2,1)S(1)}, bf16[1,14,7168]{2,1,0:T(8,128)(2,1)}, u32[]{:S(2)}) copy-start(bf16[1,14,7168]{2,1,0:T(8,128)(2,1)} %param.13) | copy-start | bytes 602116
  23.7 7.3 %copy-start.2 = (bf16[1,14,7168]{2,1,0:T(8,128)(2,1)S(1)}, bf16[1,14,7168]{2,1,0:T(8,128)(2,1)}, u32[]{:S(2)}) copy-start(bf16[1,14,7168]{2,1,0:T(8,128)(2,1)} %param.14) | copy-start | bytes 602116
  23.7 47.6 %collective-permute-start = (f32[14,2,1792]{2,0,1:T(8,128)S(1)}, f32[14,2,1792]{2,0,1:T(8,128)S(1)}, u32[]{:S(2)}, u32[]{:S(2)}) collective-permute-start(f32[14,2,1792]{2,0,1:T(8,128)S(1)} %pad_maximum_fusion), channel_id=1, source_target_pairs={{0,512},{512,0},{1,513},{513,1},{2,514},{514,2},{3,515},{515,3},{4... | collective-permute-start | bytes 602120 | tf_op jit(solution)/shard_map/ppermute | solution.py:48
  33.8 35.2 %all-to-all-start.1 = ((f32[256,1,2]{2,1,0:T(1,128)}), f32[256,1,2]{2,1,0:T(1,128)S(1)}, u32[]{:S(2)}, u32[]{:S(2)}) async-start(f32[256,1,2]{2,1,0:T(1,128)} %broadcast_in_dim.2), calls=%async_computation.1 | async-start | bytes 262144 | tf_op jit(solution)/shard_map/all_to_all | solution.py:20
  77.6 1.5 %copy-start.6 = (f32[1,14,7168]{2,0,1:T(1,128)S(1)}, f32[1,14,7168]{2,0,1:T(1,128)}, u32[]{:S(2)}) copy-start(f32[1,14,7168]{2,0,1:T(1,128)} %param.11) | copy-start | bytes 1204228
  77.9 1.1 %copy-start.1 = (f32[1,14,7168]{2,0,1:T(1,128)S(1)}, f32[1,14,7168]{2,0,1:T(1,128)}, u32[]{:S(2)}) copy-start(f32[1,14,7168]{2,0,1:T(1,128)} %param.10) | copy-start | bytes 1204228
  77.9 1.1 %copy-start.5 = (f32[1,14,7168]{2,0,1:T(1,128)S(1)}, f32[1,14,7168]{2,0,1:T(1,128)}, u32[]{:S(2)}) copy-start(f32[1,14,7168]{2,0,1:T(1,128)} %param.12) | copy-start | bytes 1204228

commit v4 on v2

--- a/solution.py
+++ b/solution.py
@@ -38,7 +38,9 @@
     hi = lax.axis_index("z_hi")
     lo = lax.axis_index("core")
     pseudo = (anchor - inner_weight[0]).reshape(rows, 2, 2, block)
-    on_chip = lax.all_to_all(pseudo, "core", 2, 2, tiled=True).sum(axis=2)
+    kept = lax.dynamic_index_in_dim(pseudo, lo, 2, keepdims=False)
+    given = lax.dynamic_index_in_dim(pseudo, 1 - lo, 2, keepdims=False)
+    on_chip = kept + lax.ppermute(given, "core", [(0, 1), (1, 0)])
     anchor_half = lax.dynamic_index_in_dim(anchor.reshape(rows, 2, 2, block), lo, 2, keepdims=False)
     own_sum = lax.dynamic_index_in_dim(on_chip, hi, 1, keepdims=False)
     other_sum = lax.dynamic_index_in_dim(on_chip, 1 - hi, 1, keepdims=False)
@@ -60,7 +62,8 @@
     base_step = 2 * outer_step[0]
     grad_one = grad_first[0].astype(jnp.float32)
     grad_two = grad_second[0].astype(jnp.float32)
-    squares = jnp.stack([jnp.sum(grad_one * grad_one), jnp.sum(grad_two * grad_two)])
+    both_grads = jnp.stack([grad_one, grad_two])
+    squares = jnp.sum(both_grads * both_grads, axis=(1, 2))
     norm_one, norm_two = all_summed(squares, FSDP)
     weight, moment_one, moment_two = adam_apply(
         inner_weight[0],

time: 82.6 us -> 91.1 us (1.10)
  the two profiles are of different devices: /device:TPU:249 before, /device:TPU:65 now
where the time goes in v4:
time: 91.1 us; the launch traced here: 90.7 us
  blocking collectives  31.5 us (35%)
  starting transfers between devices  28.1 us (31%)
  waiting for transfers between devices  15.1 us (17%)
  local copies, waits for them, and re-layouts  8.72 us (10%)
  other arithmetic  4.18 us (5%)
  between operations  3.17 us (3%)
    all_gather x1, blocking collectives, outer_update(): both = lax.all_gather(payload, 'z_hi', axis=0, tiled=False)  29.1 us
    all_to_all x1, starting transfers between devices, all_summed(): return lax.all_to_all(spread, axes, 0, 0, tiled=False).sum(axis=0)  25.4 us
    all_to_all x1, waiting for transfers between devices, all_summed(): return lax.all_to_all(spread, axes, 0, 0, tiled=False).sum(axis=0)  15.1 us
    unnamed x20, local copies, waits for them, and re-layouts  5.74 us
    ppermute x1, starting transfers between devices, outer_update(): on_chip = kept + lax.ppermute(given, 'core', [(0, 1), (1, 0)])  2.72 us
    all_gather x1, blocking collectives, outer_update(): lax.all_gather(anchor_half, 'core', axis=2, tiled=False).reshape(rows, cols)  2.45 us
  transfers between devices with their start and end apart: 2, of which 1 were waited for; matrix products, arithmetic and copies ran while one was open for 3% of the time, Pallas kernels for 0%

profile of v4, /device:TPU:65, one launch (start us, length us, event | category | flops | bytes accessed | tf_op | source)
XLA Modules:
  0.0 90.7 jit_solution(10590309211604429016)
XLA Ops:
  0.6 1.2 %fusion.1 = f32[14,7168]{1,0:T(8,128)S(1)} fusion(f32[14,7168]{1,0:T(8,128)} %param.8, f32[1,14,7168]{2,0,1:T(1,128)} %param.10), kind=kLoop, calls=%fused_computation.8 | loop fusion | flops 100352 | bytes 1204224 | tf_op jit(solution)/shard_map/sub | solution.py:40
  1.9 0.3 reshape.112
  2.2 0.4 constant_dynamic-slice_fusion.3
  2.6 0.0 copy-start.2
  2.6 2.7 %collective-permute-start = (f32[14,2,1792]{2,0,1:T(8,128)S(1)}, f32[14,2,1792]{2,0,1:T(8,128)S(1)}, u32[]{:S(2)}, u32[]{:S(2)}) collective-permute-start(f32[14,2,1792]{2,0,1:T(8,128)S(1)} %bitcast.45), channel_id=1, source_target_pairs={{0,256},{256,0},{1,257},{257,1},{2,258},{258,2},{3,259},{259,3},{4... | collective-permute-start | bytes 602120 | tf_op jit(solution)/shard_map/ppermute | solution.py:43
  5.5 0.2 fusion
  5.7 0.7 broadcast_in_dim.2
  6.4 25.4 %all-to-all-start = ((f32[256,1,2]{2,1,0:T(1,128)}), f32[256,1,2]{2,1,0:T(1,128)S(1)}, u32[]{:S(2)}, u32[]{:S(2)}) async-start(f32[256,1,2]{2,1,0:T(1,128)} %broadcast_in_dim.2), calls=%async_computation | async-start | bytes 262144 | tf_op jit(solution)/shard_map/all_to_all | solution.py:20
  31.8 0.3 reshape.111
  32.2 0.1 constant_dynamic-slice_fusion.4
  33.1 15.1 %all-to-all-done = f32[256,1,2]{2,1,0:T(1,128)S(1)} async-done(((f32[256,1,2]{2,1,0:T(1,128)}), f32[256,1,2]{2,1,0:T(1,128)S(1)}, u32[]{:S(2)}, u32[]{:S(2)}) %all-to-all-start) | async-done | bytes 2080 | tf_op jit(solution)/shard_map/all_to_all | solution.py:20
  48.2 0.3 reduce_sum.19
  48.5 0.6 fusion.17
  50.6 0.0 copy-start.4
  50.6 0.1 broadcast_multiply_fusion
  50.7 0.8 copy-done.4
  51.5 0.2 copy.73
  51.7 29.1 %all-gather = f32[28,2,1792]{2,1,0:T(2,128)S(1)} all-gather(f32[14,2,1792]{2,1,0:T(2,128)S(1)} %copy.73), channel_id=2, replica_groups=mesh['z_hi'=2,'core'=2,'fsdp_0'=8,'fsdp_1'=8,'fsdp_2'=4] {'z_hi'}, dimensions={0}, use_global_device_ids=true | all-gather | bytes 602112 | tf_op jit(solution)/shard_map/all_gather | solution.py:50
  80.8 0.3 fusion.15
  81.1 0.2 pad_maximum_fusion.1
  81.3 2.5 %all-gather.1 = f32[14,2,3584]{2,1,0:T(2,128)S(1)} all-gather(f32[14,2,1792]{2,1,0:T(2,128)S(1)} %pad_maximum_fusion.1), channel_id=3, replica_groups=mesh['z_hi'=2,'core'=2,'fsdp_0'=8,'fsdp_1'=8,'fsdp_2'=4] {'core'}, dimensions={2}, use_global_device_ids=true | all-gather | bytes 602112 | tf_op jit(solution)/shard_map/all_gather | solution.py:54
  83.7 0.1 pad.6
  83.9 0.3 reshape.114
  84.2 0.2 fusion.12
  84.4 0.7 bitcast_add_fusion
  85.1 0.9 copy.93
  86.0 0.2 copy-done.1
  86.2 0.3 copy-done.5
  86.4 0.8 fusion.6
  87.3 1.2 %copy.82 = f32[1,14,7168]{2,0,1:T(1,128)} copy(f32[1,14,7168]{2,1,0:T(8,128)S(1)} %get-tuple-element.25) | data formatting | bytes 802816
  88.4 1.2 %copy.80 = f32[1,14,7168]{2,0,1:T(1,128)} copy(f32[1,14,7168]{2,1,0:T(8,128)S(1)} %get-tuple-element.26) | data formatting | bytes 802816
  89.6 1.2 %copy.81 = f32[1,14,7168]{2,0,1:T(1,128)} copy(f32[1,14,7168]{2,1,0:T(8,128)S(1)} %get-tuple-element.27) | data formatting | bytes 802816
  (18 shorter events, 0.2 us)
Async XLA Ops:
  2.6 2.8 %copy-start.3 = (bf16[1,14,7168]{2,1,0:T(8,128)(2,1)S(1)}, bf16[1,14,7168]{2,1,0:T(8,128)(2,1)}, u32[]{:S(2)}) copy-start(bf16[1,14,7168]{2,1,0:T(8,128)(2,1)} %param.13) | copy-start | bytes 602116
  2.6 2.8 %copy-start.2 = (bf16[1,14,7168]{2,1,0:T(8,128)(2,1)S(1)}, bf16[1,14,7168]{2,1,0:T(8,128)(2,1)}, u32[]{:S(2)}) copy-start(bf16[1,14,7168]{2,1,0:T(8,128)(2,1)} %param.14) | copy-start | bytes 602116
  2.6 47.9 %collective-permute-start = (f32[14,2,1792]{2,0,1:T(8,128)S(1)}, f32[14,2,1792]{2,0,1:T(8,128)S(1)}, u32[]{:S(2)}, u32[]{:S(2)}) collective-permute-start(f32[14,2,1792]{2,0,1:T(8,128)S(1)} %bitcast.45), channel_id=1, source_target_pairs={{0,256},{256,0},{1,257},{257,1},{2,258},{258,2},{3,259},{259,3},{4... | collective-permute-start | bytes 602120 | tf_op jit(solution)/shard_map/ppermute | solution.py:43
  5.5 26.4 %copy-start = (f32[14,7168]{1,0:T(8,128)S(1)}, f32[14,7168]{1,0:T(8,128)}, u32[]{:S(2)}) copy-start(f32[14,7168]{1,0:T(8,128)} %param.8) | copy-start | bytes 1204228
  6.4 41.7 %all-to-all-start = ((f32[256,1,2]{2,1,0:T(1,128)}), f32[256,1,2]{2,1,0:T(1,128)S(1)}, u32[]{:S(2)}, u32[]{:S(2)}) async-start(f32[256,1,2]{2,1,0:T(1,128)} %broadcast_in_dim.2), calls=%async_computation | async-start | bytes 262144 | tf_op jit(solution)/shard_map/all_to_all | solution.py:20
  50.6 0.9 copy-start.4
  84.4 1.5 %copy-start.6 = (f32[1,14,7168]{2,0,1:T(1,128)S(1)}, f32[1,14,7168]{2,0,1:T(1,128)}, u32[]{:S(2)}) copy-start(f32[1,14,7168]{2,0,1:T(1,128)} %param.11) | copy-start | bytes 1204228
  85.1 1.1 %copy-start.1 = (f32[1,14,7168]{2,0,1:T(1,128)S(1)}, f32[1,14,7168]{2,0,1:T(1,128)}, u32[]{:S(2)}) copy-start(f32[1,14,7168]{2,0,1:T(1,128)} %param.10) | copy-start | bytes 1204228
  85.1 1.3 %copy-start.5 = (f32[1,14,7168]{2,0,1:T(1,128)S(1)}, f32[1,14,7168]{2,0,1:T(1,128)}, u32[]{:S(2)}) copy-start(f32[1,14,7168]{2,0,1:T(1,128)} %param.12) | copy-start | bytes 1204228

commit v5 on v2

--- a/solution.py
+++ b/solution.py
@@ -60,7 +60,8 @@
     base_step = 2 * outer_step[0]
     grad_one = grad_first[0].astype(jnp.float32)
     grad_two = grad_second[0].astype(jnp.float32)
-    squares = jnp.stack([jnp.sum(grad_one * grad_one), jnp.sum(grad_two * grad_two)])
+    both_grads = jnp.stack([grad_one, grad_two])
+    squares = jnp.sum(both_grads * both_grads, axis=(1, 2))
     norm_one, norm_two = all_summed(squares, FSDP)
     weight, moment_one, moment_two = adam_apply(
         inner_weight[0],

time: 82.6 us -> 81 us (0.981)
  other arithmetic: 6.86 us -> 4.35 us
  local copies, waits for them, and re-layouts: 9.64 us -> 10.5 us
    another operation x1 -> x0, other arithmetic: 1.37 us -> none  [inner_steps(): jnp.stack([jnp.sum(grad_one * grad_one), jnp.sum(grad_two * grad_two)])]
    reduce_sum x2 -> x1, other arithmetic: 1.44 us -> 0.23 us  [inner_steps(): squares = jnp.sum(both_grads * both_grads, axis=(1, 2))]
    unnamed x19, local copies, waits for them, and re-layouts: 5.89 us -> 6.8 us
  transfers between devices with their start and end apart: 2 -> 2, of which waited for: 0 -> 0; matrix products, arithmetic and copies ran while one was open for 8% -> 5% of each run, Pallas kernels for 0% -> 0%
where the time goes in v5:
time: 81 us; the launch traced here: 80.6 us
  blocking collectives  34.1 us (42%)
  starting transfers between devices  28.5 us (35%)
  local copies, waits for them, and re-layouts  10.5 us (13%)
  other arithmetic  4.35 us (5%)
  between operations  3.1 us (4%)
    all_gather x1, blocking collectives, outer_update(): both = lax.all_gather(payload, 'z_hi', axis=0, tiled=False)  31.7 us
    all_to_all x1, starting transfers between devices, all_summed(): return lax.all_to_all(spread, axes, 0, 0, tiled=False).sum(axis=0)  24.2 us
    unnamed x19, local copies, waits for them, and re-layouts  6.8 us
    all_to_all x1, starting transfers between devices, outer_update(): on_chip = lax.all_to_all(pseudo, 'core', 2, 2, tiled=True).sum(axis=2)  4.26 us
    all_gather x1, blocking collectives, outer_update(): lax.all_gather(anchor_half, 'core', axis=2, tiled=False).reshape(rows, cols)  2.38 us
  transfers between devices with their start and end apart: 2, of which 0 were waited for; matrix products, arithmetic and copies ran while one was open for 5% of the time, Pallas kernels for 0%

profile of v5, /device:TPU:249, one launch (start us, length us, event | category | flops | bytes accessed | tf_op | source)
XLA Modules:
  0.0 80.6 jit_solution(17701947631709736809)
XLA Ops:
  0.6 1.2 %fusion.1 = f32[14,7168]{1,0:T(8,128)S(1)} fusion(f32[14,7168]{1,0:T(8,128)} %param.8, f32[1,14,7168]{2,0,1:T(1,128)} %param.10), kind=kLoop, calls=%fused_computation.8 | loop fusion | flops 100352 | bytes 1204224 | tf_op jit(solution)/shard_map/sub | solution.py:40
  1.9 0.3 reshape.112
  2.2 1.0 %copy.76 = f32[14,2,2,1792]{3,1,0,2:T(2,128)} copy(f32[14,2,2,1792]{3,2,1,0:T(2,128)S(1)} %reshape.112) | data formatting | bytes 802816 | tf_op jit(solution)/shard_map/reshape | solution.py:40
  3.2 4.3 %all-to-all-start = ((f32[14,2,2,1792]{3,1,0,2:T(2,128)}), f32[14,2,2,1792]{3,1,0,2:T(2,128)S(1)}, u32[]{:S(2)}, u32[]{:S(2)}) async-start(f32[14,2,2,1792]{3,1,0,2:T(2,128)} %copy.76), calls=%async_computation | async-start | bytes 802816 | tf_op jit(solution)/shard_map/all_to_all | solution.py:41
  7.4 0.3 reshape.111
  7.8 0.6 copy-done.3
  8.4 0.9 %copy-done.2 = bf16[1,14,7168]{2,1,0:T(8,128)(2,1)S(1)} copy-done((bf16[1,14,7168]{2,1,0:T(8,128)(2,1)S(1)}, bf16[1,14,7168]{2,1,0:T(8,128)(2,1)}, u32[]{:S(2)}) %copy-start.2) | copy-done | bytes 200728
  9.3 0.2 fusion
  9.6 0.7 broadcast_in_dim.2
  10.3 24.2 %all-to-all-start.1 = ((f32[256,1,2]{2,1,0:T(1,128)}), f32[256,1,2]{2,1,0:T(1,128)S(1)}, u32[]{:S(2)}, u32[]{:S(2)}) async-start(f32[256,1,2]{2,1,0:T(1,128)} %broadcast_in_dim.2), calls=%async_computation.1 | async-start | bytes 262144 | tf_op jit(solution)/shard_map/all_to_all | solution.py:20
  34.6 0.3 reduce_sum.27
  34.9 0.2 constant_dynamic-slice_fusion.1
  35.1 0.0 copy-start.4
  35.1 0.1 constant_dynamic-slice_fusion.2
  35.2 0.8 copy-done.4
  36.0 0.1 stack.8
  36.1 0.2 pad_maximum_fusion
  36.3 31.7 %all-gather = f32[28,2,1792]{2,1,0:T(2,128)S(1)} all-gather(f32[14,2,1792]{2,1,0:T(2,128)S(1)} %pad_maximum_fusion), channel_id=2, replica_groups=mesh['z_hi'=2,'core'=2,'fsdp_0'=8,'fsdp_1'=8,'fsdp_2'=4] {'z_hi'}, dimensions={0}, use_global_device_ids=true | all-gather | bytes 602112 | tf_op jit(solution)/shard_map/all_gather | solution.py:48
  68.0 0.3 fusion.16
  68.3 0.1 slice.24
  68.4 0.7 fusion.12
  69.1 0.2 pad_maximum_fusion.1
  69.3 2.4 %all-gather.1 = f32[14,2,3584]{2,1,0:T(2,128)S(1)} all-gather(f32[14,2,1792]{2,1,0:T(2,128)S(1)} %pad_maximum_fusion.1), channel_id=3, replica_groups=mesh['z_hi'=2,'core'=2,'fsdp_0'=8,'fsdp_1'=8,'fsdp_2'=4] {'core'}, dimensions={2}, use_global_device_ids=true | all-gather | bytes 602112 | tf_op jit(solution)/shard_map/all_gather | solution.py:52
  72.5 0.2 pad.6
  72.7 0.3 reshape.114
  73.0 0.9 %copy.97 = f32[2,8,2,3584]{3,1,2,0:T(8,128)} copy(f32[2,8,2,3584]{3,2,1,0:T(2,128)S(1)} %bitcast.36) | data formatting | bytes 917504
  73.9 0.3 reduce_sum.29
  74.2 0.6 fusion.18
  76.3 0.8 %fusion.6 = (f32[1,14,7168]{2,1,0:T(8,128)S(1)}, f32[1,14,7168]{2,1,0:T(8,128)S(1)}, f32[1,14,7168]{2,1,0:T(8,128)S(1)}) fusion(f32[]{:T(128)} %bitcast.10, bf16[1,14,7168]{2,1,0:T(8,128)(2,1)S(1)} %copy-done.2, bf16[1,14,7168]{2,1,0:T(8,128)(2,1)S(1)} %copy-done.3, f32[]{:T(128)} %bitcast.7, f32[1,14,7168]{2,0,1:T(1,128)S(1)} %copy-done.5, ...), kind=kLoop, calls=%fused_computation.13 | loop fusion | flops 3612672 | bytes 3211288 | tf_op jit(solution)/shard_map/add | solution.py:27
  77.1 1.2 %copy.88 = f32[1,14,7168]{2,0,1:T(1,128)} copy(f32[1,14,7168]{2,1,0:T(8,128)S(1)} %get-tuple-element.30) | data formatting | bytes 802816
  78.3 1.2 %copy.86 = f32[1,14,7168]{2,0,1:T(1,128)} copy(f32[1,14,7168]{2,1,0:T(8,128)S(1)} %get-tuple-element.31) | data formatting | bytes 802816
  79.4 1.2 %copy.87 = f32[1,14,7168]{2,0,1:T(1,128)} copy(f32[1,14,7168]{2,1,0:T(8,128)S(1)} %get-tuple-element.32) | data formatting | bytes 802816
  (16 shorter events, 0.1 us)
Async XLA Ops:
  3.2 4.3 %copy-start = (f32[14,7168]{1,0:T(8,128)S(1)}, f32[14,7168]{1,0:T(8,128)}, u32[]{:S(2)}) copy-start(f32[14,7168]{1,0:T(8,128)} %param.8) | copy-start | bytes 1204228
  3.2 6.4 %all-to-all-start = ((f32[14,2,2,1792]{3,1,0,2:T(2,128)}), f32[14,2,2,1792]{3,1,0,2:T(2,128)S(1)}, u32[]{:S(2)}, u32[]{:S(2)}) async-start(f32[14,2,2,1792]{3,1,0,2:T(2,128)} %copy.76), calls=%async_computation | async-start | bytes 802816 | tf_op jit(solution)/shard_map/all_to_all | solution.py:41
  7.4 0.9 %copy-start.3 = (bf16[1,14,7168]{2,1,0:T(8,128)(2,1)S(1)}, bf16[1,14,7168]{2,1,0:T(8,128)(2,1)}, u32[]{:S(2)}) copy-start(bf16[1,14,7168]{2,1,0:T(8,128)(2,1)} %param.13) | copy-start | bytes 602116
  8.4 0.9 %copy-start.2 = (bf16[1,14,7168]{2,1,0:T(8,128)(2,1)S(1)}, bf16[1,14,7168]{2,1,0:T(8,128)(2,1)}, u32[]{:S(2)}) copy-start(bf16[1,14,7168]{2,1,0:T(8,128)(2,1)} %param.14) | copy-start | bytes 602116
  10.3 63.6 %all-to-all-start.1 = ((f32[256,1,2]{2,1,0:T(1,128)}), f32[256,1,2]{2,1,0:T(1,128)S(1)}, u32[]{:S(2)}, u32[]{:S(2)}) async-start(f32[256,1,2]{2,1,0:T(1,128)} %broadcast_in_dim.2), calls=%async_computation.1 | async-start | bytes 262144 | tf_op jit(solution)/shard_map/all_to_all | solution.py:20
  35.1 0.9 %copy-start.4 = (f32[14,1792]{1,0:T(8,128)S(1)}, f32[14,1792]{1,0:T(8,128)}, u32[]{:S(2)}) copy-start(f32[14,1792]{1,0:T(8,128)} %param.9) | copy-start | bytes 301060
  72.7 3.6 %copy-start.6 = (f32[1,14,7168]{2,0,1:T(1,128)S(1)}, f32[1,14,7168]{2,0,1:T(1,128)}, u32[]{:S(2)}) copy-start(f32[1,14,7168]{2,0,1:T(1,128)} %param.11) | copy-start | bytes 1204228
  73.0 3.2 %copy-start.1 = (f32[1,14,7168]{2,0,1:T(1,128)S(1)}, f32[1,14,7168]{2,0,1:T(1,128)}, u32[]{:S(2)}) copy-start(f32[1,14,7168]{2,0,1:T(1,128)} %param.10) | copy-start | bytes 1204228
  73.0 3.2 %copy-start.5 = (f32[1,14,7168]{2,0,1:T(1,128)S(1)}, f32[1,14,7168]{2,0,1:T(1,128)}, u32[]{:S(2)}) copy-start(f32[1,14,7168]{2,0,1:T(1,128)} %param.12) | copy-start | bytes 1204228

commit v6 on v4

--- a/solution.py
+++ b/solution.py
@@ -40,7 +40,10 @@
     pseudo = (anchor - inner_weight[0]).reshape(rows, 2, 2, block)
     kept = lax.dynamic_index_in_dim(pseudo, lo, 2, keepdims=False)
     given = lax.dynamic_index_in_dim(pseudo, 1 - lo, 2, keepdims=False)
-    on_chip = kept + lax.ppermute(given, "core", [(0, 1), (1, 0)])
+    from_sibling = lax.dynamic_index_in_dim(
+        lax.all_gather(given, "core", axis=0, tiled=False), 1 - lo, 0, keepdims=False
+    )
+    on_chip = kept + from_sibling
     anchor_half = lax.dynamic_index_in_dim(anchor.reshape(rows, 2, 2, block), lo, 2, keepdims=False)
     own_sum = lax.dynamic_index_in_dim(on_chip, hi, 1, keepdims=False)
     other_sum = lax.dynamic_index_in_dim(on_chip, 1 - hi, 1, keepdims=False)

time: 91.1 us -> 73.7 us (0.81)
  the two profiles are of different devices: /device:TPU:65 before, /device:TPU:121 now
where the time goes in v6:
time: 73.7 us; the launch traced here: 73.4 us
  blocking collectives  30.9 us (42%)
  starting transfers between devices  26 us (35%)
  local copies, waits for them, and re-layouts  9.24 us (13%)
  other arithmetic  4.01 us (5%)
  between operations  3.15 us (4%)
    all_to_all x1, starting transfers between devices, all_summed(): return lax.all_to_all(spread, axes, 0, 0, tiled=False).sum(axis=0)  26 us
    all_gather x1, blocking collectives, outer_update(): both = lax.all_gather(payload, 'z_hi', axis=0, tiled=False)  23.9 us
    unnamed x19, local copies, waits for them, and re-layouts  5.98 us
    all_gather x1, blocking collectives, outer_update(): lax.all_gather(anchor_half, 'core', axis=2, tiled=False).reshape(rows, cols)  4.11 us
    all_gather x1, blocking collectives, outer_update(): lax.all_gather(given, 'core', axis=0, tiled=False)  2.96 us
  transfers between devices with their start and end apart: 1, of which 0 were waited for; matrix products, arithmetic and copies ran while one was open for 6% of the time, Pallas kernels for 0%

profile of v6, /device:TPU:121, one launch (start us, length us, event | category | flops | bytes accessed | tf_op | source)
XLA Modules:
  0.0 73.4 jit_solution(3181131629641329482)
XLA Ops:
  0.6 1.0 %convert_element_type.22 = f32[1,14,7168]{2,1,0:T(8,128)S(1)} convert(bf16[1,14,7168]{2,1,0:T(8,128)(2,1)} %param.13) | non-fusion elementwise | flops 100352 | bytes 602112 | tf_op jit(solution)/shard_map/convert_element_type | solution.py:66
  1.7 0.2 fusion
  2.0 0.7 broadcast_in_dim.2
  2.7 26.0 %all-to-all-start = ((f32[256,1,2]{2,1,0:T(1,128)}), f32[256,1,2]{2,1,0:T(1,128)S(1)}, u32[]{:S(2)}, u32[]{:S(2)}) async-start(f32[256,1,2]{2,1,0:T(1,128)} %broadcast_in_dim.2), calls=%async_computation | async-start | bytes 262144 | tf_op jit(solution)/shard_map/all_to_all | solution.py:20
  28.8 0.3 reshape.112
  29.1 0.6 copy-done.1
  29.7 0.1 fusion.1
  29.8 0.3 reshape.113
  30.2 0.4 constant_dynamic-slice_fusion.2
  30.5 0.1 copy.78
  30.7 3.0 %all-gather = f32[28,2,1,1792]{3,1,2,0:T(2,128)S(1)} all-gather(f32[14,2,1,1792]{3,1,2,0:T(2,128)S(1)} %copy.78), channel_id=2, replica_groups=mesh['z_hi'=2,'core'=2,'fsdp_0'=8,'fsdp_1'=8,'fsdp_2'=4] {'core'}, dimensions={0}, use_global_device_ids=true | all-gather | bytes 602112 | tf_op jit(solution)/shard_map/all_gather | solution.py:44
  33.6 0.1 bitcast_add_fusion
  33.8 0.2 constant_dynamic-slice_fusion.1
  34.0 0.1 constant_dynamic-slice_fusion.4
  34.1 0.8 %copy-done.4 = f32[14,1792]{1,0:T(8,128)S(1)} copy-done((f32[14,1792]{1,0:T(8,128)S(1)}, f32[14,1792]{1,0:T(8,128)}, u32[]{:S(2)}) %copy-start.4) | copy-done | bytes 100376
  34.9 0.1 stack.8
  35.0 0.2 pad_maximum_fusion
  35.2 23.9 %all-gather.1 = f32[28,2,1792]{2,1,0:T(2,128)S(1)} all-gather(f32[14,2,1792]{2,1,0:T(2,128)S(1)} %pad_maximum_fusion), channel_id=3, replica_groups=mesh['z_hi'=2,'core'=2,'fsdp_0'=8,'fsdp_1'=8,'fsdp_2'=4] {'z_hi'}, dimensions={0}, use_global_device_ids=true | all-gather | bytes 602112 | tf_op jit(solution)/shard_map/all_gather | solution.py:53
  59.1 0.3 fusion.16
  59.3 0.1 slice.24
  59.5 0.7 fusion.12
  60.1 0.2 pad_maximum_fusion.1
  60.3 4.1 %all-gather.2 = f32[14,2,3584]{2,1,0:T(2,128)S(1)} all-gather(f32[14,2,1792]{2,1,0:T(2,128)S(1)} %pad_maximum_fusion.1), channel_id=4, replica_groups=mesh['z_hi'=2,'core'=2,'fsdp_0'=8,'fsdp_1'=8,'fsdp_2'=4] {'core'}, dimensions={2}, use_global_device_ids=true | all-gather | bytes 602112 | tf_op jit(solution)/shard_map/all_gather | solution.py:57
  65.2 0.3 reshape.115
  65.6 0.2 pad.6
  65.8 0.9 %copy.98 = f32[2,8,2,3584]{3,1,2,0:T(8,128)} copy(f32[2,8,2,3584]{3,2,1,0:T(2,128)S(1)} %bitcast.41) | data formatting | bytes 917504
  66.7 0.3 reduce_sum.19
  66.9 0.6 fusion.18
  69.0 0.8 %fusion.6 = (f32[1,14,7168]{2,1,0:T(8,128)S(1)}, f32[1,14,7168]{2,1,0:T(8,128)S(1)}, f32[1,14,7168]{2,1,0:T(8,128)S(1)}) fusion(f32[]{:T(128)} %bitcast.12, bf16[1,14,7168]{2,1,0:T(8,128)(2,1)S(1)} %copy-done.2, bf16[1,14,7168]{2,1,0:T(8,128)(2,1)S(1)} %copy-done.3, f32[]{:T(128)} %bitcast.9, f32[1,14,7168]{2,0,1:T(1,128)S(1)} %copy-done.5, ...), kind=kLoop, calls=%fused_computation.13 | loop fusion | flops 3612672 | bytes 3211288 | tf_op jit(solution)/shard_map/add | solution.py:27
  69.9 1.2 %copy.89 = f32[1,14,7168]{2,0,1:T(1,128)} copy(f32[1,14,7168]{2,1,0:T(8,128)S(1)} %get-tuple-element.30) | data formatting | bytes 802816
  71.0 1.2 %copy.87 = f32[1,14,7168]{2,0,1:T(1,128)} copy(f32[1,14,7168]{2,1,0:T(8,128)S(1)} %get-tuple-element.31) | data formatting | bytes 802816
  72.2 1.2 %copy.88 = f32[1,14,7168]{2,0,1:T(1,128)} copy(f32[1,14,7168]{2,1,0:T(8,128)S(1)} %get-tuple-element.32) | data formatting | bytes 802816
  (16 shorter events, 0.1 us)
Async XLA Ops:
  0.6 1.0 %copy-start.2 = (bf16[1,14,7168]{2,1,0:T(8,128)(2,1)S(1)}, bf16[1,14,7168]{2,1,0:T(8,128)(2,1)}, u32[]{:S(2)}) copy-start(bf16[1,14,7168]{2,1,0:T(8,128)(2,1)} %param.14) | copy-start | bytes 602116
  1.7 27.0 %copy-start = (f32[14,7168]{1,0:T(8,128)S(1)}, f32[14,7168]{1,0:T(8,128)}, u32[]{:S(2)}) copy-start(f32[14,7168]{1,0:T(8,128)} %param.8) | copy-start | bytes 1204228
  2.7 64.0 %all-to-all-start = ((f32[256,1,2]{2,1,0:T(1,128)}), f32[256,1,2]{2,1,0:T(1,128)S(1)}, u32[]{:S(2)}, u32[]{:S(2)}) async-start(f32[256,1,2]{2,1,0:T(1,128)} %broadcast_in_dim.2), calls=%async_computation | async-start | bytes 262144 | tf_op jit(solution)/shard_map/all_to_all | solution.py:20
  28.7 1.0 %copy-start.1 = (f32[1,14,7168]{2,0,1:T(1,128)S(1)}, f32[1,14,7168]{2,0,1:T(1,128)}, u32[]{:S(2)}) copy-start(f32[1,14,7168]{2,0,1:T(1,128)} %param.10) | copy-start | bytes 1204228
  33.9 0.9 %copy-start.4 = (f32[14,1792]{1,0:T(8,128)S(1)}, f32[14,1792]{1,0:T(8,128)}, u32[]{:S(2)}) copy-start(f32[14,1792]{1,0:T(8,128)} %param.9) | copy-start | bytes 301060
  65.8 3.2 %copy-start.3 = (bf16[1,14,7168]{2,1,0:T(8,128)(2,1)S(1)}, bf16[1,14,7168]{2,1,0:T(8,128)(2,1)}, u32[]{:S(2)}) copy-start(bf16[1,14,7168]{2,1,0:T(8,128)(2,1)} %param.13) | copy-start | bytes 602116
  65.8 3.2 %copy-start.5 = (f32[1,14,7168]{2,0,1:T(1,128)S(1)}, f32[1,14,7168]{2,0,1:T(1,128)}, u32[]{:S(2)}) copy-start(f32[1,14,7168]{2,0,1:T(1,128)} %param.12) | copy-start | bytes 1204228
  65.8 3.2 %copy-start.6 = (f32[1,14,7168]{2,0,1:T(1,128)S(1)}, f32[1,14,7168]{2,0,1:T(1,128)}, u32[]{:S(2)}) copy-start(f32[1,14,7168]{2,0,1:T(1,128)} %param.11) | copy-start | bytes 1204228

commit v7 on v6

--- a/solution.py
+++ b/solution.py
@@ -50,12 +50,18 @@
     own_anchor = lax.dynamic_index_in_dim(anchor_half, hi, 1, keepdims=False)
     folded = own_anchor - 0.567 * momentum - 0.3325 * own_sum
     payload = jnp.stack([folded, other_sum], axis=1)
-    both = lax.all_gather(payload, "z_hi", axis=0, tiled=False)
-    anchor_half = jnp.stack(
-        [both[0, :, 0] - 0.3325 * both[1, :, 1], both[1, :, 0] - 0.3325 * both[0, :, 1]], axis=1
-    )
-    next_anchor = lax.all_gather(anchor_half, "core", axis=2, tiled=False).reshape(rows, cols)
-    arrived = lax.dynamic_index_in_dim(both, 1 - hi, 0, keepdims=False)[:, 1]
+    every = lax.all_gather(payload, REP, axis=0, tiled=False).reshape(2, 2, rows, 2, block)
+    next_anchor = jnp.stack(
+        [
+            jnp.stack(
+                [every[h, c, :, 0] - 0.3325 * every[1 - h, c, :, 1] for c in range(2)], axis=1
+            )
+            for h in range(2)
+        ],
+        axis=1,
+    ).reshape(rows, cols)
+    partner = lax.dynamic_index_in_dim(every, 1 - hi, 0, keepdims=False)
+    arrived = lax.dynamic_index_in_dim(partner, lo, 0, keepdims=False)[:, 1]
     outer_grad = (own_sum + arrived) / replicas
     next_momentum = 0.9 * momentum + outer_grad
     return (next_anchor, next_momentum)

time: 73.7 us -> 73.4 us (level)
  blocking collectives: 30.9 us -> 29.9 us
    reshape x1 -> x2, local copies, waits for them, and re-layouts: 0.35 us -> 1.41 us  [outer_update(): next_anchor = jnp.stack([jnp.stack([every[h, c, :, 0] - 0.3325 * every[1...]
    unnamed x19 -> x17, local copies, waits for them, and re-layouts: 5.98 us -> 4.97 us
    all_gather x2 -> x1, blocking collectives: 28 us -> 27 us  [outer_update(): lax.all_gather(payload, REP, axis=0, tiled=False)]
  transfers between devices with their start and end apart: 1 -> 1, of which waited for: 0 -> 0; matrix products, arithmetic and copies ran while one was open for 6% -> 7% of each run, Pallas kernels for 0% -> 0%
where the time goes in v7:
time: 73.4 us; the launch traced here: 73.1 us
  blocking collectives  29.9 us (41%)
  starting transfers between devices  26 us (35%)
  local copies, waits for them, and re-layouts  9.34 us (13%)
  other arithmetic  4.66 us (6%)
  between operations  3.15 us (4%)
    all_gather x1, blocking collectives, outer_update(): lax.all_gather(payload, REP, axis=0, tiled=False)  27 us
    all_to_all x1, starting transfers between devices, all_summed(): return lax.all_to_all(spread, axes, 0, 0, tiled=False).sum(axis=0)  26 us
    unnamed x17, local copies, waits for them, and re-layouts  4.97 us
    all_gather x1, blocking collectives, outer_update(): lax.all_gather(given, 'core', axis=0, tiled=False)  2.96 us
  transfers between devices with their start and end apart: 1, of which 0 were waited for; matrix products, arithmetic and copies ran while one was open for 7% of the time, Pallas kernels for 0%

profile of v7, /device:TPU:121, one launch (start us, length us, event | category | flops | bytes accessed | tf_op | source)
XLA Modules:
  0.0 73.1 jit_solution(17890049802079362203)
XLA Ops:
  0.6 1.0 %convert_element_type.22 = f32[1,14,7168]{2,1,0:T(8,128)S(1)} convert(bf16[1,14,7168]{2,1,0:T(8,128)(2,1)} %param.13) | non-fusion elementwise | flops 100352 | bytes 602112 | tf_op jit(solution)/shard_map/convert_element_type | solution.py:72
  1.7 0.0 copy-done.2
  1.7 0.2 fusion
  2.0 0.7 broadcast_in_dim.2
  2.7 26.0 %all-to-all-start = ((f32[256,1,2]{2,1,0:T(1,128)}), f32[256,1,2]{2,1,0:T(1,128)S(1)}, u32[]{:S(2)}, u32[]{:S(2)}) async-start(f32[256,1,2]{2,1,0:T(1,128)} %broadcast_in_dim.2), calls=%async_computation | async-start | bytes 262144 | tf_op jit(solution)/shard_map/all_to_all | solution.py:20
  28.8 0.3 reshape.163
  29.1 0.6 copy-done.1
  29.7 0.1 fusion.1
  29.8 0.3 reshape.164
  30.2 0.4 constant_dynamic-slice_fusion.2
  30.5 0.1 copy.90
  30.7 3.0 %all-gather = f32[28,2,1,1792]{3,1,2,0:T(2,128)S(1)} all-gather(f32[14,2,1,1792]{3,1,2,0:T(2,128)S(1)} %copy.90), channel_id=2, replica_groups=mesh['z_hi'=2,'core'=2,'fsdp_0'=8,'fsdp_1'=8,'fsdp_2'=4] {'core'}, dimensions={0}, use_global_device_ids=true | all-gather | bytes 602112 | tf_op jit(solution)/shard_map/all_gather | solution.py:44
  33.6 0.1 bitcast_add_fusion
  33.8 0.2 constant_dynamic-slice_fusion.1
  34.0 0.1 constant_dynamic-slice_fusion.4
  34.1 0.8 %copy-done.4 = f32[14,1792]{1,0:T(8,128)S(1)} copy-done((f32[14,1792]{1,0:T(8,128)S(1)}, f32[14,1792]{1,0:T(8,128)}, u32[]{:S(2)}) %copy-start.4) | copy-done | bytes 100376
  34.9 0.1 stack.31
  35.0 0.2 pad_maximum_fusion.1
  35.2 27.0 %all-gather.1 = f32[56,2,1792]{2,1,0:T(2,128)S(1)} all-gather(f32[14,2,1792]{2,1,0:T(2,128)S(1)} %pad_maximum_fusion.1), channel_id=3, replica_groups=mesh['z_hi'=2,'core'=2,'fsdp_0'=8,'fsdp_1'=8,'fsdp_2'=4] {'z_hi','core'}, dimensions={0}, use_global_device_ids=true | all-gather | bytes 1003520 | tf_op jit(solution)/shard_map/all_gather | solution.py:53
  62.1 0.6 fusion.18
  62.8 0.1 slice.44
  62.9 0.7 fusion.12
  63.5 0.4 maximum_bitcast_fusion
  63.9 0.2 pad_maximum_fusion
  65.0 0.3 reshape.167
  65.3 1.1 %reshape.166 = f32[14,7168]{1,0:T(8,128)} reshape(f32[14,2,2,1792]{3,2,1,0:T(2,128)S(1)} %copy.92) | data formatting | bytes 802816 | tf_op jit(solution)/shard_map/reshape | solution.py:62
  66.4 0.3 reduce_sum.19
  66.7 0.6 fusion.22
  68.8 0.8 %fusion.6 = (f32[1,14,7168]{2,1,0:T(8,128)S(1)}, f32[1,14,7168]{2,1,0:T(8,128)S(1)}, f32[1,14,7168]{2,1,0:T(8,128)S(1)}) fusion(f32[]{:T(128)} %bitcast.16, bf16[1,14,7168]{2,1,0:T(8,128)(2,1)S(1)} %copy-done.2, bf16[1,14,7168]{2,1,0:T(8,128)(2,1)S(1)} %copy-done.3, f32[]{:T(128)} %bitcast.13, f32[1,14,7168]{2,0,1:T(1,128)S(1)} %copy-done.5, ...), kind=kLoop, calls=%fused_computation.13 | loop fusion | flops 3612672 | bytes 3211288 | tf_op jit(solution)/shard_map/add | solution.py:27
  69.6 1.2 %copy.103 = f32[1,14,7168]{2,0,1:T(1,128)} copy(f32[1,14,7168]{2,1,0:T(8,128)S(1)} %get-tuple-element.30) | data formatting | bytes 802816
  70.8 1.2 %copy.101 = f32[1,14,7168]{2,0,1:T(1,128)} copy(f32[1,14,7168]{2,1,0:T(8,128)S(1)} %get-tuple-element.31) | data formatting | bytes 802816
  72.0 1.2 %copy.102 = f32[1,14,7168]{2,0,1:T(1,128)} copy(f32[1,14,7168]{2,1,0:T(8,128)S(1)} %get-tuple-element.32) | data formatting | bytes 802816
  (16 shorter events, 0.2 us)
Async XLA Ops:
  0.6 1.0 %copy-start.2 = (bf16[1,14,7168]{2,1,0:T(8,128)(2,1)S(1)}, bf16[1,14,7168]{2,1,0:T(8,128)(2,1)}, u32[]{:S(2)}) copy-start(bf16[1,14,7168]{2,1,0:T(8,128)(2,1)} %param.14) | copy-start | bytes 602116
  1.7 27.0 %copy-start = (f32[14,7168]{1,0:T(8,128)S(1)}, f32[14,7168]{1,0:T(8,128)}, u32[]{:S(2)}) copy-start(f32[14,7168]{1,0:T(8,128)} %param.8) | copy-start | bytes 1204228
  2.7 63.7 %all-to-all-start = ((f32[256,1,2]{2,1,0:T(1,128)}), f32[256,1,2]{2,1,0:T(1,128)S(1)}, u32[]{:S(2)}, u32[]{:S(2)}) async-start(f32[256,1,2]{2,1,0:T(1,128)} %broadcast_in_dim.2), calls=%async_computation | async-start | bytes 262144 | tf_op jit(solution)/shard_map/all_to_all | solution.py:20
  28.7 1.0 %copy-start.1 = (f32[1,14,7168]{2,0,1:T(1,128)S(1)}, f32[1,14,7168]{2,0,1:T(1,128)}, u32[]{:S(2)}) copy-start(f32[1,14,7168]{2,0,1:T(1,128)} %param.10) | copy-start | bytes 1204228
  33.9 0.9 %copy-start.4 = (f32[14,1792]{1,0:T(8,128)S(1)}, f32[14,1792]{1,0:T(8,128)}, u32[]{:S(2)}) copy-start(f32[14,1792]{1,0:T(8,128)} %param.9) | copy-start | bytes 301060
  65.3 3.5 %copy-start.3 = (bf16[1,14,7168]{2,1,0:T(8,128)(2,1)S(1)}, bf16[1,14,7168]{2,1,0:T(8,128)(2,1)}, u32[]{:S(2)}) copy-start(bf16[1,14,7168]{2,1,0:T(8,128)(2,1)} %param.13) | copy-start | bytes 602116
  65.3 3.5 %copy-start.5 = (f32[1,14,7168]{2,0,1:T(1,128)S(1)}, f32[1,14,7168]{2,0,1:T(1,128)}, u32[]{:S(2)}) copy-start(f32[1,14,7168]{2,0,1:T(1,128)} %param.12) | copy-start | bytes 1204228
  65.3 3.5 %copy-start.6 = (f32[1,14,7168]{2,0,1:T(1,128)S(1)}, f32[1,14,7168]{2,0,1:T(1,128)}, u32[]{:S(2)}) copy-start(f32[1,14,7168]{2,0,1:T(1,128)} %param.11) | copy-start | bytes 1204228

commit v8 on v5

--- a/solution.py
+++ b/solution.py
@@ -37,20 +37,28 @@
     block = cols // replicas
     hi = lax.axis_index("z_hi")
     lo = lax.axis_index("core")
-    pseudo = (anchor - inner_weight[0]).reshape(rows, 2, 2, block)
-    on_chip = lax.all_to_all(pseudo, "core", 2, 2, tiled=True).sum(axis=2)
-    anchor_half = lax.dynamic_index_in_dim(anchor.reshape(rows, 2, 2, block), lo, 2, keepdims=False)
-    own_sum = lax.dynamic_index_in_dim(on_chip, hi, 1, keepdims=False)
-    other_sum = lax.dynamic_index_in_dim(on_chip, 1 - hi, 1, keepdims=False)
-    own_anchor = lax.dynamic_index_in_dim(anchor_half, hi, 1, keepdims=False)
-    folded = own_anchor - 0.567 * momentum - 0.3325 * own_sum
-    payload = jnp.stack([folded, other_sum], axis=1)
-    both = lax.all_gather(payload, "z_hi", axis=0, tiled=False)
-    anchor_half = jnp.stack(
-        [both[0, :, 0] - 0.3325 * both[1, :, 1], both[1, :, 0] - 0.3325 * both[0, :, 1]], axis=1
+
+    def column(x, b):
+        return lax.dynamic_slice_in_dim(x, b * block, block, 1)
+
+    pseudo = anchor - inner_weight[0]
+    kept = jnp.concatenate([column(pseudo, lo), column(pseudo, 2 + lo)], axis=1)
+    given = jnp.concatenate([column(pseudo, 1 - lo), column(pseudo, 3 - lo)], axis=1)
+    sibling = lax.all_gather(given, "core", axis=0, tiled=False)
+    on_chip = kept + lax.dynamic_index_in_dim(sibling, 1 - lo, 0, keepdims=False)
+    own_sum = column(on_chip, hi)
+    other_sum = column(on_chip, 1 - hi)
+    folded = column(anchor, 2 * hi + lo) - 0.567 * momentum - 0.3325 * own_sum
+    payload = jnp.concatenate([folded, other_sum], axis=1)
+    every = lax.all_gather(payload, REP, axis=0, tiled=False)
+    next_anchor = jnp.concatenate(
+        [
+            every[b, :, :block] - 0.3325 * every[(b + 2) % 4, :, block:]
+            for b in range(replicas)
+        ],
+        axis=1,
     )
-    next_anchor = lax.all_gather(anchor_half, "core", axis=2, tiled=False).reshape(rows, cols)
-    arrived = lax.dynamic_index_in_dim(both, 1 - hi, 0, keepdims=False)[:, 1]
+    arrived = lax.dynamic_index_in_dim(every, 2 * (1 - hi) + lo, 0, keepdims=False)[:, block:]
     outer_grad = (own_sum + arrived) / replicas
     next_momentum = 0.9 * momentum + outer_grad
     return (next_anchor, next_momentum)

time: 81 us -> 75.5 us (0.932)
  the two profiles are of different devices: /device:TPU:249 before, /device:TPU:121 now
where the time goes in v8:
time: 75.5 us; the launch traced here: 75.2 us
  blocking collectives  36.2 us (48%)
  starting transfers between devices  26 us (34%)
  local copies, waits for them, and re-layouts  5.78 us (8%)
  other arithmetic  4.16 us (6%)
  between operations  3.07 us (4%)
    all_gather x1, blocking collectives, outer_update(): every = lax.all_gather(payload, REP, axis=0, tiled=False)  33.2 us
    all_to_all x1, starting transfers between devices, all_summed(): return lax.all_to_all(spread, axes, 0, 0, tiled=False).sum(axis=0)  26 us
    unnamed x17, local copies, waits for them, and re-layouts  4.4 us
    all_gather x1, blocking collectives, outer_update(): sibling = lax.all_gather(given, 'core', axis=0, tiled=False)  3 us
  transfers between devices with their start and end apart: 1, of which 0 were waited for; matrix products, arithmetic and copies ran while one was open for 2% of the time, Pallas kernels for 0%

profile of v8, /device:TPU:121, one launch (start us, length us, event | category | flops | bytes accessed | tf_op | source)
XLA Modules:
  0.0 75.2 jit_solution(15215547503687603870)
XLA Ops:
  0.6 0.0 copy-start.1
  0.6 1.0 %convert_element_type.22 = f32[1,14,7168]{2,1,0:T(8,128)S(1)} convert(bf16[1,14,7168]{2,1,0:T(8,128)(2,1)} %param.13) | non-fusion elementwise | flops 100352 | bytes 602112 | tf_op jit(solution)/shard_map/convert_element_type | solution.py:69
  1.7 0.0 copy-done.1
  1.7 0.0 copy-start.3
  1.7 0.2 fusion
  2.0 0.0 copy-start
  2.0 0.7 broadcast_in_dim.2
  2.7 26.0 %all-to-all-start = ((f32[256,1,2]{2,1,0:T(1,128)}), f32[256,1,2]{2,1,0:T(1,128)S(1)}, u32[]{:S(2)}, u32[]{:S(2)}) async-start(f32[256,1,2]{2,1,0:T(1,128)} %broadcast_in_dim.2), calls=%async_computation | async-start | bytes 262144 | tf_op jit(solution)/shard_map/all_to_all | solution.py:20
  28.7 0.0 copy-done.3
  28.7 0.0 copy-done
  28.8 0.1 fusion.1
  28.9 3.0 %all-gather.2 = f32[2,14,3584]{2,1,0:T(8,128)S(1)} all-gather(f32[1,14,3584]{2,1,0:T(8,128)S(1)} %maximum_bitcast_fusion), channel_id=2, replica_groups=mesh['z_hi'=2,'core'=2,'fsdp_0'=8,'fsdp_1'=8,'fsdp_2'=4] {'core'}, dimensions={0}, use_global_device_ids=true | all-gather | bytes 602112 | tf_op jit(solution)/shard_map/all_gather | solution.py:47
  31.9 0.0 copy-start.4
  32.0 0.9 %copy-done.4 = f32[14,1792]{1,0:T(8,128)S(1)} copy-done((f32[14,1792]{1,0:T(8,128)S(1)}, f32[14,1792]{1,0:T(8,128)}, u32[]{:S(2)}) %copy-start.4) | copy-done | bytes 100376
  32.9 33.2 %all-gather.3 = f32[4,14,3584]{2,1,0:T(8,128)S(1)} all-gather(f32[1,14,3584]{2,1,0:T(8,128)S(1)} %maximum_bitcast_fusion.1), channel_id=3, replica_groups=mesh['z_hi'=2,'core'=2,'fsdp_0'=8,'fsdp_1'=8,'fsdp_2'=4] {'z_hi','core'}, dimensions={0}, use_global_device_ids=true | all-gather | bytes 1003520 | tf_op jit(solution)/shard_map/all_gather | solution.py:53
  66.1 0.1 fusion.13
  66.2 0.0 copy-start.6
  66.2 0.8 %pad_maximum_fusion = f32[14,7168]{1,0:T(8,128)} fusion(f32[14,1792]{1,0:T(8,128)S(1)} %bitcast.25, f32[14,1792]{1,0:T(8,128)S(1)} %bitcast.24, f32[14,1792]{1,0:T(8,128)S(1)} %bitcast.23, f32[14,1792]{1,0:T(8,128)S(1)} %bitcast.22), kind=kLoop, calls=%fused_computation.14 | loop fusion | flops 301056 | bytes 802816 | tf_op jit(solution)/shard_map/concatenate | solution.py:54
  67.0 0.0 copy-start.2
  67.0 0.0 copy-start.5
  67.0 0.7 fusion.9
  68.5 0.0 all-to-all-done
  68.5 0.3 reduce_sum.19
  68.8 0.6 fusion.14
  70.8 0.0 copy-done.6
  70.8 0.0 copy-done.2
  70.8 0.0 copy-done.5
  70.8 0.9 %fusion.6 = (f32[1,14,7168]{2,1,0:T(8,128)S(1)}, f32[1,14,7168]{2,1,0:T(8,128)S(1)}, f32[1,14,7168]{2,1,0:T(8,128)S(1)}) fusion(f32[]{:T(128)} %bitcast.11, bf16[1,14,7168]{2,1,0:T(8,128)(2,1)S(1)} %copy-done.1, bf16[1,14,7168]{2,1,0:T(8,128)(2,1)S(1)} %copy-done.2, f32[]{:T(128)} %bitcast.8, f32[1,14,7168]{2,0,1:T(1,128)S(1)} %copy-done.5, f32[]{:T(128)} %bitcast.13, ...), kind=kLoop, calls=%fused_computation.13 | loop fusion | flops 3913728 | bytes 3211288 | tf_op jit(solution)/shard_map/add | solution.py:27
  71.7 1.2 %copy.44 = f32[1,14,7168]{2,0,1:T(1,128)} copy(f32[1,14,7168]{2,1,0:T(8,128)S(1)} %get-tuple-element.24) | data formatting | bytes 802816
  72.9 1.2 %copy.42 = f32[1,14,7168]{2,0,1:T(1,128)} copy(f32[1,14,7168]{2,1,0:T(8,128)S(1)} %get-tuple-element.25) | data formatting | bytes 802816
  74.0 1.2 %copy.43 = f32[1,14,7168]{2,0,1:T(1,128)} copy(f32[1,14,7168]{2,1,0:T(8,128)S(1)} %get-tuple-element.26) | data formatting | bytes 802816
  (7 shorter events, 0.2 us)
Async XLA Ops:
  0.6 1.0 %copy-start.1 = (bf16[1,14,7168]{2,1,0:T(8,128)(2,1)S(1)}, bf16[1,14,7168]{2,1,0:T(8,128)(2,1)}, u32[]{:S(2)}) copy-start(bf16[1,14,7168]{2,1,0:T(8,128)(2,1)} %param.14) | copy-start | bytes 602116
  1.7 27.0 %copy-start.3 = (f32[14,7168]{1,0:T(8,128)S(1)}, f32[14,7168]{1,0:T(8,128)}, u32[]{:S(2)}) copy-start(f32[14,7168]{1,0:T(8,128)} %param.8) | copy-start | bytes 1204228
  2.0 26.8 %copy-start = (f32[1,14,7168]{2,0,1:T(1,128)S(1)}, f32[1,14,7168]{2,0,1:T(1,128)}, u32[]{:S(2)}) copy-start(f32[1,14,7168]{2,0,1:T(1,128)} %param.10) | copy-start | bytes 1204228
  2.7 65.8 %all-to-all-start = ((f32[256,1,2]{2,1,0:T(1,128)}), f32[256,1,2]{2,1,0:T(1,128)S(1)}, u32[]{:S(2)}, u32[]{:S(2)}) async-start(f32[256,1,2]{2,1,0:T(1,128)} %broadcast_in_dim.2), calls=%async_computation | async-start | bytes 262144 | tf_op jit(solution)/shard_map/all_to_all | solution.py:20
  31.9 0.9 %copy-start.4 = (f32[14,1792]{1,0:T(8,128)S(1)}, f32[14,1792]{1,0:T(8,128)}, u32[]{:S(2)}) copy-start(f32[14,1792]{1,0:T(8,128)} %param.9) | copy-start | bytes 301060
  66.2 4.7 %copy-start.6 = (f32[1,14,7168]{2,0,1:T(1,128)S(1)}, f32[1,14,7168]{2,0,1:T(1,128)}, u32[]{:S(2)}) copy-start(f32[1,14,7168]{2,0,1:T(1,128)} %param.11) | copy-start | bytes 1204228
  67.0 3.9 %copy-start.2 = (bf16[1,14,7168]{2,1,0:T(8,128)(2,1)S(1)}, bf16[1,14,7168]{2,1,0:T(8,128)(2,1)}, u32[]{:S(2)}) copy-start(bf16[1,14,7168]{2,1,0:T(8,128)(2,1)} %param.13) | copy-start | bytes 602116
  67.0 3.9 %copy-start.5 = (f32[1,14,7168]{2,0,1:T(1,128)S(1)}, f32[1,14,7168]{2,0,1:T(1,128)}, u32[]{:S(2)}) copy-start(f32[1,14,7168]{2,0,1:T(1,128)} %param.12) | copy-start | bytes 1204228

commit v9 on v8

--- a/solution.py
+++ b/solution.py
@@ -66,10 +66,11 @@
 
 def inner_steps(inner_weight, first_moment, second_moment, grad_first, grad_second, outer_step):
     base_step = 2 * outer_step[0]
+    both_grads = jnp.concatenate([grad_first, grad_second]).astype(jnp.float32)
+    squares = jnp.sum(both_grads * both_grads, axis=(1, 2))
+    grad_first, grad_second = lax.optimization_barrier((grad_first, grad_second))
     grad_one = grad_first[0].astype(jnp.float32)
     grad_two = grad_second[0].astype(jnp.float32)
-    both_grads = jnp.stack([grad_one, grad_two])
-    squares = jnp.sum(both_grads * both_grads, axis=(1, 2))
     norm_one, norm_two = all_summed(squares, FSDP)
     weight, moment_one, moment_two = adam_apply(
         inner_weight[0],

time: 75.5 us -> 75.5 us (level)
    reduce_sum x1, other arithmetic: 0.23 us -> 1.38 us  [inner_steps(): squares = jnp.sum(both_grads * both_grads, axis=(1, 2))]
    convert_element_type x2 -> x0, other arithmetic: 1.04 us -> none  [the longest x1 1.01 us: inner_steps(): grad_one = grad_first[0].astype(jnp.float32)]
where the time goes in v9:
time: 75.5 us; the launch traced here: 75.3 us
  blocking collectives  36.2 us (48%)
  starting transfers between devices  26 us (34%)
  local copies, waits for them, and re-layouts  5.76 us (8%)
  other arithmetic  4.26 us (6%)
  between operations  3.08 us (4%)
    all_gather x1, blocking collectives, outer_update(): every = lax.all_gather(payload, REP, axis=0, tiled=False)  33.2 us
    all_to_all x1, starting transfers between devices, all_summed(): return lax.all_to_all(spread, axes, 0, 0, tiled=False).sum(axis=0)  26 us
    unnamed x17, local copies, waits for them, and re-layouts  4.38 us
    all_gather x1, blocking collectives, outer_update(): sibling = lax.all_gather(given, 'core', axis=0, tiled=False)  3 us
  transfers between devices with their start and end apart: 1, of which 0 were waited for; matrix products, arithmetic and copies ran while one was open for 2% of the time, Pallas kernels for 0%

profile of v9, /device:TPU:121, one launch (start us, length us, event | category | flops | bytes accessed | tf_op | source)
XLA Modules:
  0.0 75.3 jit_solution(11495056888331549857)
XLA Ops:
  0.6 0.0 copy-start
  0.6 0.0 copy-start.3
  0.7 1.4 %multiply_reduce_fusion = f32[2]{0:T(128)S(1)} fusion(bf16[1,14,7168]{2,1,0:T(8,128)(2,1)} %param.14, bf16[1,14,7168]{2,1,0:T(8,128)(2,1)} %param.13), kind=kLoop, calls=%fused_computation | loop fusion | flops 802814 | bytes 401416 | tf_op jit(solution)/shard_map/reduce_sum | solution.py:70
  2.0 0.7 broadcast_in_dim.2
  2.8 26.0 %all-to-all-start = ((f32[256,1,2]{2,1,0:T(1,128)}), f32[256,1,2]{2,1,0:T(1,128)S(1)}, u32[]{:S(2)}, u32[]{:S(2)}) async-start(f32[256,1,2]{2,1,0:T(1,128)} %broadcast_in_dim.2), calls=%async_computation | async-start | bytes 262144 | tf_op jit(solution)/shard_map/all_to_all | solution.py:20
  28.8 0.0 copy-done
  28.8 0.0 copy-done.3
  28.8 0.1 fusion
  29.0 3.0 %all-gather.2 = f32[2,14,3584]{2,1,0:T(8,128)S(1)} all-gather(f32[1,14,3584]{2,1,0:T(8,128)S(1)} %maximum_bitcast_fusion), channel_id=2, replica_groups=mesh['z_hi'=2,'core'=2,'fsdp_0'=8,'fsdp_1'=8,'fsdp_2'=4] {'core'}, dimensions={0}, use_global_device_ids=true | all-gather | bytes 602112 | tf_op jit(solution)/shard_map/all_gather | solution.py:47
  32.0 0.0 copy-start.4
  32.0 0.9 %copy-done.4 = f32[14,1792]{1,0:T(8,128)S(1)} copy-done((f32[14,1792]{1,0:T(8,128)S(1)}, f32[14,1792]{1,0:T(8,128)}, u32[]{:S(2)}) %copy-start.4) | copy-done | bytes 100376
  33.0 33.2 %all-gather.3 = f32[4,14,3584]{2,1,0:T(8,128)S(1)} all-gather(f32[1,14,3584]{2,1,0:T(8,128)S(1)} %maximum_bitcast_fusion.1), channel_id=3, replica_groups=mesh['z_hi'=2,'core'=2,'fsdp_0'=8,'fsdp_1'=8,'fsdp_2'=4] {'z_hi','core'}, dimensions={0}, use_global_device_ids=true | all-gather | bytes 1003520 | tf_op jit(solution)/shard_map/all_gather | solution.py:53
  66.1 0.1 fusion.12
  66.2 0.0 copy-start.5
  66.2 0.0 copy-start.6
  66.3 0.8 %pad_maximum_fusion = f32[14,7168]{1,0:T(8,128)} fusion(f32[14,1792]{1,0:T(8,128)S(1)} %bitcast.25, f32[14,1792]{1,0:T(8,128)S(1)} %bitcast.24, f32[14,1792]{1,0:T(8,128)S(1)} %bitcast.23, f32[14,1792]{1,0:T(8,128)S(1)} %bitcast.22), kind=kLoop, calls=%fused_computation.13 | loop fusion | flops 301056 | bytes 802816 | tf_op jit(solution)/shard_map/concatenate | solution.py:54
  67.1 0.0 copy-start.1
  67.1 0.0 copy-start.2
  67.1 0.7 fusion.8
  68.6 0.0 all-to-all-done
  68.6 0.3 reduce_sum.19
  68.8 0.6 fusion.13
  70.9 0.0 copy-done.5
  70.9 0.0 copy-done.6
  70.9 0.0 copy-done.1
  70.9 0.0 copy-done.2
  70.9 0.9 %fusion.5 = (f32[1,14,7168]{2,1,0:T(8,128)S(1)}, f32[1,14,7168]{2,1,0:T(8,128)S(1)}, f32[1,14,7168]{2,1,0:T(8,128)S(1)}) fusion(bf16[1,14,7168]{2,1,0:T(8,128)(2,1)S(1)} %copy-done.1, f32[]{:T(128)} %bitcast.11, bf16[1,14,7168]{2,1,0:T(8,128)(2,1)S(1)} %copy-done.2, f32[1,14,7168]{2,0,1:T(1,128)S(1)} %copy-done.5, f32[]{:T(128)} %bitcast.8, f32[]{:T(128)} %bitcast.13, ...), kind=kLoop, calls=%fused_computation.12 | loop fusion | flops 3913728 | bytes 3211288 | tf_op jit(solution)/shard_map/add | solution.py:27
  71.8 1.2 %copy.44 = f32[1,14,7168]{2,0,1:T(1,128)} copy(f32[1,14,7168]{2,1,0:T(8,128)S(1)} %get-tuple-element.28) | data formatting | bytes 802816
  73.0 1.2 %copy.42 = f32[1,14,7168]{2,0,1:T(1,128)} copy(f32[1,14,7168]{2,1,0:T(8,128)S(1)} %get-tuple-element.29) | data formatting | bytes 802816
  74.1 1.2 %copy.43 = f32[1,14,7168]{2,0,1:T(1,128)} copy(f32[1,14,7168]{2,1,0:T(8,128)S(1)} %get-tuple-element.30) | data formatting | bytes 802816
  (6 shorter events, 0.2 us)
Async XLA Ops:
  0.6 28.2 %copy-start = (f32[1,14,7168]{2,0,1:T(1,128)S(1)}, f32[1,14,7168]{2,0,1:T(1,128)}, u32[]{:S(2)}) copy-start(f32[1,14,7168]{2,0,1:T(1,128)} %param.10) | copy-start | bytes 1204228
  0.6 28.2 %copy-start.3 = (f32[14,7168]{1,0:T(8,128)S(1)}, f32[14,7168]{1,0:T(8,128)}, u32[]{:S(2)}) copy-start(f32[14,7168]{1,0:T(8,128)} %param.8) | copy-start | bytes 1204228
  2.8 65.8 %all-to-all-start = ((f32[256,1,2]{2,1,0:T(1,128)}), f32[256,1,2]{2,1,0:T(1,128)S(1)}, u32[]{:S(2)}, u32[]{:S(2)}) async-start(f32[256,1,2]{2,1,0:T(1,128)} %broadcast_in_dim.2), calls=%async_computation | async-start | bytes 262144 | tf_op jit(solution)/shard_map/all_to_all | solution.py:20
  32.0 0.9 %copy-start.4 = (f32[14,1792]{1,0:T(8,128)S(1)}, f32[14,1792]{1,0:T(8,128)}, u32[]{:S(2)}) copy-start(f32[14,1792]{1,0:T(8,128)} %param.9) | copy-start | bytes 301060
  66.2 4.7 %copy-start.5 = (f32[1,14,7168]{2,0,1:T(1,128)S(1)}, f32[1,14,7168]{2,0,1:T(1,128)}, u32[]{:S(2)}) copy-start(f32[1,14,7168]{2,0,1:T(1,128)} %param.12) | copy-start | bytes 1204228
  66.2 4.7 %copy-start.6 = (f32[1,14,7168]{2,0,1:T(1,128)S(1)}, f32[1,14,7168]{2,0,1:T(1,128)}, u32[]{:S(2)}) copy-start(f32[1,14,7168]{2,0,1:T(1,128)} %param.11) | copy-start | bytes 1204228
  67.1 3.9 %copy-start.1 = (bf16[1,14,7168]{2,1,0:T(8,128)(2,1)S(1)}, bf16[1,14,7168]{2,1,0:T(8,128)(2,1)}, u32[]{:S(2)}) copy-start(bf16[1,14,7168]{2,1,0:T(8,128)(2,1)} %param.14) | copy-start | bytes 602116
  67.1 3.9 %copy-start.2 = (bf16[1,14,7168]{2,1,0:T(8,128)(2,1)S(1)}, bf16[1,14,7168]{2,1,0:T(8,128)(2,1)}, u32[]{:S(2)}) copy-start(bf16[1,14,7168]{2,1,0:T(8,128)(2,1)} %param.13) | copy-start | bytes 602116

commit v10 on v9

--- a/solution.py
+++ b/solution.py
@@ -42,23 +42,19 @@
         return lax.dynamic_slice_in_dim(x, b * block, block, 1)
 
     pseudo = anchor - inner_weight[0]
-    kept = jnp.concatenate([column(pseudo, lo), column(pseudo, 2 + lo)], axis=1)
-    given = jnp.concatenate([column(pseudo, 1 - lo), column(pseudo, 3 - lo)], axis=1)
+    kept = jnp.stack([column(pseudo, lo), column(pseudo, 2 + lo)], axis=1)
+    given = jnp.stack([column(pseudo, 1 - lo), column(pseudo, 3 - lo)], axis=1)
     sibling = lax.all_gather(given, "core", axis=0, tiled=False)
     on_chip = kept + lax.dynamic_index_in_dim(sibling, 1 - lo, 0, keepdims=False)
-    own_sum = column(on_chip, hi)
-    other_sum = column(on_chip, 1 - hi)
+    own_sum = lax.dynamic_index_in_dim(on_chip, hi, 1, keepdims=False)
+    other_sum = lax.dynamic_index_in_dim(on_chip, 1 - hi, 1, keepdims=False)
     folded = column(anchor, 2 * hi + lo) - 0.567 * momentum - 0.3325 * own_sum
-    payload = jnp.concatenate([folded, other_sum], axis=1)
+    payload = jnp.stack([folded, other_sum], axis=1)
     every = lax.all_gather(payload, REP, axis=0, tiled=False)
     next_anchor = jnp.concatenate(
-        [
-            every[b, :, :block] - 0.3325 * every[(b + 2) % 4, :, block:]
-            for b in range(replicas)
-        ],
-        axis=1,
+        [every[b, :, 0] - 0.3325 * every[(b + 2) % 4, :, 1] for b in range(replicas)], axis=1
     )
-    arrived = lax.dynamic_index_in_dim(every, 2 * (1 - hi) + lo, 0, keepdims=False)[:, block:]
+    arrived = lax.dynamic_index_in_dim(every, 2 * (1 - hi) + lo, 0, keepdims=False)[:, 1]
     outer_grad = (own_sum + arrived) / replicas
     next_momentum = 0.9 * momentum + outer_grad
     return (next_anchor, next_momentum)

time: 75.5 us -> 75.4 us (level)
  other arithmetic: 4.26 us -> 12.8 us
  blocking collectives: 36.2 us -> 30.1 us
  local copies, waits for them, and re-layouts: 5.76 us -> 2.99 us
    add x1, other arithmetic: 0.86 us -> 8.14 us  [on_device(): next_inner = (next_anchor + (weight - inner_weight[0]))[None]]
    all_gather x1, blocking collectives: 33.2 us -> 27.2 us  [outer_update(): every = lax.all_gather(payload, REP, axis=0, tiled=False)]
    unnamed x17 -> x15, local copies, waits for them, and re-layouts: 4.38 us -> 0.76 us
  transfers between devices with their start and end apart: 1 -> 1, of which waited for: 0 -> 0; matrix products, arithmetic and copies ran while one was open for 2% -> 5% of each run, Pallas kernels for 0% -> 0%
where the time goes in v10:
time: 75.4 us; the launch traced here: 75.1 us
  blocking collectives  30.1 us (40%)
  starting transfers between devices  26 us (34%)
  other arithmetic  12.8 us (17%)
  between operations  3.19 us (4%)
  local copies, waits for them, and re-layouts  2.99 us (4%)
    all_gather x1, blocking collectives, outer_update(): every = lax.all_gather(payload, REP, axis=0, tiled=False)  27.2 us
    all_to_all x1, starting transfers between devices, all_summed(): return lax.all_to_all(spread, axes, 0, 0, tiled=False).sum(axis=0)  26 us
    add x1, other arithmetic, on_device(): next_inner = (next_anchor + (weight - inner_weight[0]))[None]  8.14 us
    all_gather x1, blocking collectives, outer_update(): sibling = lax.all_gather(given, 'core', axis=0, tiled=False)  2.96 us
  transfers between devices with their start and end apart: 1, of which 0 were waited for; matrix products, arithmetic and copies ran while one was open for 5% of the time, Pallas kernels for 0%

profile of v10, /device:TPU:121, one launch (start us, length us, event | category | flops | bytes accessed | tf_op | source)
XLA Modules:
  0.0 75.1 jit_solution(5276578711447742383)
XLA Ops:
  0.7 1.4 %multiply_reduce_fusion = f32[2]{0:T(128)S(1)} fusion(bf16[1,14,7168]{2,1,0:T(8,128)(2,1)} %param.14, bf16[1,14,7168]{2,1,0:T(8,128)(2,1)} %param.13), kind=kLoop, calls=%fused_computation | loop fusion | flops 802814 | bytes 401416 | tf_op jit(solution)/shard_map/reduce_sum | solution.py:66
  2.0 0.7 broadcast_in_dim.2
  2.8 26.0 %all-to-all-start = ((f32[256,1,2]{2,1,0:T(1,128)}), f32[256,1,2]{2,1,0:T(1,128)S(1)}, u32[]{:S(2)}, u32[]{:S(2)}) async-start(f32[256,1,2]{2,1,0:T(1,128)} %broadcast_in_dim.2), calls=%async_computation | async-start | bytes 262144 | tf_op jit(solution)/shard_map/all_to_all | solution.py:20
  28.8 0.1 bitcast_subtract_fusion
  29.0 0.1 stack.28
  29.1 0.1 stack.29
  29.1 0.1 stack.26
  29.2 0.1 stack.25
  29.3 0.2 pad_maximum_fusion.1
  29.5 3.0 %all-gather = f32[28,2,1792]{2,1,0:T(2,128)S(1)} all-gather(f32[14,2,1792]{2,1,0:T(2,128)S(1)} %pad_maximum_fusion.1), channel_id=2, replica_groups=mesh['z_hi'=2,'core'=2,'fsdp_0'=8,'fsdp_1'=8,'fsdp_2'=4] {'core'}, dimensions={0}, use_global_device_ids=true | all-gather | bytes 602112 | tf_op jit(solution)/shard_map/all_gather | solution.py:47
  32.4 0.2 maximum_add_fusion.1
  32.7 0.0 copy-start.4
  32.7 0.2 constant_dynamic-slice_fusion.1
  32.9 0.7 copy-done.4
  33.6 0.1 stack.31
  33.7 0.2 pad_maximum_fusion.2
  33.9 27.2 %all-gather.1 = f32[56,2,1792]{2,1,0:T(2,128)S(1)} all-gather(f32[14,2,1792]{2,1,0:T(2,128)S(1)} %pad_maximum_fusion.2), channel_id=3, replica_groups=mesh['z_hi'=2,'core'=2,'fsdp_0'=8,'fsdp_1'=8,'fsdp_2'=4] {'z_hi','core'}, dimensions={0}, use_global_device_ids=true | all-gather | bytes 1003520 | tf_op jit(solution)/shard_map/all_gather | solution.py:53
  61.1 0.5 fusion.18
  61.6 0.1 slice.44
  61.8 0.1 fusion.12
  61.9 0.1 fusion.13
  62.0 0.0 copy-start.6
  62.0 0.8 %pad_maximum_fusion = f32[14,7168]{1,0:T(8,128)} fusion(f32[14,1792]{1,0:T(8,128)S(1)} %get-tuple-element.32, f32[14,1792]{1,0:T(8,128)S(1)} %get-tuple-element.33, f32[14,1792]{1,0:T(8,128)S(1)} %get-tuple-element.30, f32[14,1792]{1,0:T(8,128)S(1)} %get-tuple-element.23), kind=kLoop, calls=%fused_computation.3 | loop fusion | flops 301056 | bytes 802816 | tf_op jit(solution)/shard_map/concatenate | solution.py:54
  62.8 0.7 fusion.8
  64.3 0.0 copy-start.2
  64.3 0.1 copy.85
  64.4 0.0 copy-start.1
  64.5 0.1 copy.86
  64.6 0.0 all-to-all-done
  64.6 0.3 reduce_sum.19
  64.9 0.6 fusion.19
  67.0 8.1 %maximum_add_fusion = (f32[1,14,7168]{2,0,1:T(1,128)}, f32[1,14,7168]{2,0,1:T(1,128)}, f32[1,14,7168]{2,0,1:T(1,128)}) fusion(f32[1,14,1792]{2,0,1:T(1,128)S(1)} %bitcast.44, f32[1,14,1792]{2,0,1:T(1,128)S(1)} %bitcast.45, f32[1,14,1792]{2,0,1:T(1,128)S(1)} %copy.86, f32[1,14,1792]{2,0,1:T(1,128)S(1)} %copy.85, f32[1,14,7168]{2,0,1:T(1,128)S(1)} %copy-done, ...), kind=kLoop, calls=%fused_computation.7 | loop fusion | flops 3913728 | bytes 3211288 | tf_op jit(solution)/shard_map/add | solution.py:92
  (14 shorter events, 0.2 us)
Async XLA Ops:
  0.6 28.2 %copy-start = (f32[1,14,7168]{2,0,1:T(1,128)S(1)}, f32[1,14,7168]{2,0,1:T(1,128)}, u32[]{:S(2)}) copy-start(f32[1,14,7168]{2,0,1:T(1,128)} %param.10) | copy-start | bytes 1204228
  0.6 28.2 %copy-start.3 = (f32[14,7168]{1,0:T(8,128)S(1)}, f32[14,7168]{1,0:T(8,128)}, u32[]{:S(2)}) copy-start(f32[14,7168]{1,0:T(8,128)} %param.8) | copy-start | bytes 1204228
  2.8 61.8 %all-to-all-start = ((f32[256,1,2]{2,1,0:T(1,128)}), f32[256,1,2]{2,1,0:T(1,128)S(1)}, u32[]{:S(2)}, u32[]{:S(2)}) async-start(f32[256,1,2]{2,1,0:T(1,128)} %broadcast_in_dim.2), calls=%async_computation | async-start | bytes 262144 | tf_op jit(solution)/shard_map/all_to_all | solution.py:20
  32.7 0.9 %copy-start.4 = (f32[14,1792]{1,0:T(8,128)S(1)}, f32[14,1792]{1,0:T(8,128)}, u32[]{:S(2)}) copy-start(f32[14,1792]{1,0:T(8,128)} %param.9) | copy-start | bytes 301060
  62.0 4.9 %copy-start.6 = (f32[1,14,7168]{2,0,1:T(1,128)S(1)}, f32[1,14,7168]{2,0,1:T(1,128)}, u32[]{:S(2)}) copy-start(f32[1,14,7168]{2,0,1:T(1,128)} %param.12) | copy-start | bytes 1204228
  62.8 4.1 %copy-start.5 = (f32[1,14,7168]{2,0,1:T(1,128)S(1)}, f32[1,14,7168]{2,0,1:T(1,128)}, u32[]{:S(2)}) copy-start(f32[1,14,7168]{2,0,1:T(1,128)} %param.11) | copy-start | bytes 1204228
  64.3 2.6 %copy-start.2 = (bf16[1,14,7168]{2,1,0:T(8,128)(2,1)S(1)}, bf16[1,14,7168]{2,1,0:T(8,128)(2,1)}, u32[]{:S(2)}) copy-start(bf16[1,14,7168]{2,1,0:T(8,128)(2,1)} %param.14) | copy-start | bytes 602116
  64.4 2.5 %copy-start.1 = (bf16[1,14,7168]{2,1,0:T(8,128)(2,1)S(1)}, bf16[1,14,7168]{2,1,0:T(8,128)(2,1)}, u32[]{:S(2)}) copy-start(bf16[1,14,7168]{2,1,0:T(8,128)(2,1)} %param.13) | copy-start | bytes 602116

commit v11 on v7

--- a/solution.py
+++ b/solution.py
@@ -51,15 +51,10 @@
     folded = own_anchor - 0.567 * momentum - 0.3325 * own_sum
     payload = jnp.stack([folded, other_sum], axis=1)
     every = lax.all_gather(payload, REP, axis=0, tiled=False).reshape(2, 2, rows, 2, block)
-    next_anchor = jnp.stack(
-        [
-            jnp.stack(
-                [every[h, c, :, 0] - 0.3325 * every[1 - h, c, :, 1] for c in range(2)], axis=1
-            )
-            for h in range(2)
-        ],
+    next_anchor = jnp.concatenate(
+        [every[b // 2, b % 2, :, 0] - 0.3325 * every[1 - b // 2, b % 2, :, 1] for b in range(replicas)],
         axis=1,
-    ).reshape(rows, cols)
+    )
     partner = lax.dynamic_index_in_dim(every, 1 - hi, 0, keepdims=False)
     arrived = lax.dynamic_index_in_dim(partner, lo, 0, keepdims=False)[:, 1]
     outer_grad = (own_sum + arrived) / replicas

time: 73.4 us -> 77.8 us (1.060)
  other arithmetic: 4.66 us -> 13.7 us
  local copies, waits for them, and re-layouts: 9.34 us -> 4.62 us
    add x1, other arithmetic: 0.84 us -> 8.13 us  [on_device(): next_inner = (next_anchor + (weight - inner_weight[0]))[None]]
    unnamed x17 -> x16, local copies, waits for them, and re-layouts: 4.97 us -> 1.49 us
    convert_element_type x1, other arithmetic: 0.03 us -> 1.67 us  [inner_steps(): grad_two = grad_second[0].astype(jnp.float32)]
    reshape x2 -> x0, local copies, waits for them, and re-layouts: 1.41 us -> none  [outer_update(): next_anchor = jnp.stack([jnp.stack([every[h, c, :, 0] - 0.3325 * every[1...]
    convert_element_type x1 -> x0, other arithmetic: 1.01 us -> none  [inner_steps(): grad_one = grad_first[0].astype(jnp.float32)]
    concatenate x0 -> x1, other arithmetic: none -> 0.8 us  [outer_update(): jnp.concatenate([every[b // 2, b % 2, :, 0] - 0.3325 * every[1 - b // 2,...]
  transfers between devices with their start and end apart: 1 -> 1, of which waited for: 0 -> 0; matrix products, arithmetic and copies ran while one was open for 7% -> 6% of each run, Pallas kernels for 0% -> 0%
where the time goes in v11:
time: 77.8 us; the launch traced here: 77.5 us
  blocking collectives  29.9 us (38%)
  starting transfers between devices  26 us (33%)
  other arithmetic  13.7 us (18%)
  local copies, waits for them, and re-layouts  4.62 us (6%)
  between operations  3.18 us (4%)
    all_gather x1, blocking collectives, outer_update(): lax.all_gather(payload, REP, axis=0, tiled=False)  27 us
    all_to_all x1, starting transfers between devices, all_summed(): return lax.all_to_all(spread, axes, 0, 0, tiled=False).sum(axis=0)  26 us
    add x1, other arithmetic, on_device(): next_inner = (next_anchor + (weight - inner_weight[0]))[None]  8.13 us
    all_gather x1, blocking collectives, outer_update(): lax.all_gather(given, 'core', axis=0, tiled=False)  2.96 us
    convert_element_type x1, other arithmetic, inner_steps(): grad_two = grad_second[0].astype(jnp.float32)  1.67 us
  transfers between devices with their start and end apart: 1, of which 0 were waited for; matrix products, arithmetic and copies ran while one was open for 6% of the time, Pallas kernels for 0%

profile of v11, /device:TPU:121, one launch (start us, length us, event | category | flops | bytes accessed | tf_op | source)
XLA Modules:
  0.0 77.5 jit_solution(15173908646589025113)
XLA Ops:
  0.6 1.7 %copy_convert_fusion = (f32[1,14,7168]{2,0,1:T(1,128)S(1)}, f32[1,14,7168]{2,0,1:T(1,128)S(1)}) fusion(bf16[1,14,7168]{2,1,0:T(8,128)(2,1)} %param.14, bf16[1,14,7168]{2,1,0:T(8,128)(2,1)} %param.13), kind=kLoop, calls=%fused_computation.9 | loop fusion | flops 200704 | bytes 1204224 | tf_op jit(solution)/shard_map/convert_element_type | solution.py:68
  2.3 0.9 %fusion = f32[2]{0:T(128)S(1)} fusion(f32[1,14,7168]{2,0,1:T(1,128)S(1)} %get-tuple-element.26, f32[1,14,7168]{2,0,1:T(1,128)S(1)} %get-tuple-element.27), kind=kLoop, calls=%fused_computation.1 | loop fusion | flops 602110 | bytes 802824 | tf_op jit(solution)/shard_map/reduce_sum | solution.py:70
  3.3 0.7 broadcast_in_dim.2
  4.0 26.0 %all-to-all-start = ((f32[256,1,2]{2,1,0:T(1,128)}), f32[256,1,2]{2,1,0:T(1,128)S(1)}, u32[]{:S(2)}, u32[]{:S(2)}) async-start(f32[256,1,2]{2,1,0:T(1,128)} %broadcast_in_dim.2), calls=%async_computation | async-start | bytes 262144 | tf_op jit(solution)/shard_map/all_to_all | solution.py:20
  30.0 0.0 copy-start.1
  30.1 0.3 reshape.149
  30.4 0.6 copy-done.1
  31.0 0.1 bitcast_subtract_fusion
  31.1 0.3 reshape.150
  31.5 0.4 constant_dynamic-slice_fusion.2
  31.8 0.1 copy.103
  32.0 3.0 %all-gather = f32[28,2,1,1792]{3,1,2,0:T(2,128)S(1)} all-gather(f32[14,2,1,1792]{3,1,2,0:T(2,128)S(1)} %copy.103), channel_id=2, replica_groups=mesh['z_hi'=2,'core'=2,'fsdp_0'=8,'fsdp_1'=8,'fsdp_2'=4] {'core'}, dimensions={0}, use_global_device_ids=true | all-gather | bytes 602112 | tf_op jit(solution)/shard_map/all_gather | solution.py:44
  34.9 0.1 bitcast_add_fusion
  35.1 0.2 constant_dynamic-slice_fusion.1
  35.3 0.0 copy-start.4
  35.3 0.1 constant_dynamic-slice_fusion.4
  35.4 0.8 %copy-done.4 = f32[14,1792]{1,0:T(8,128)S(1)} copy-done((f32[14,1792]{1,0:T(8,128)S(1)}, f32[14,1792]{1,0:T(8,128)}, u32[]{:S(2)}) %copy-start.4) | copy-done | bytes 100376
  36.2 0.1 stack.12
  36.3 0.2 pad_maximum_fusion.1
  36.5 27.0 %all-gather.1 = f32[56,2,1792]{2,1,0:T(2,128)S(1)} all-gather(f32[14,2,1792]{2,1,0:T(2,128)S(1)} %pad_maximum_fusion.1), channel_id=3, replica_groups=mesh['z_hi'=2,'core'=2,'fsdp_0'=8,'fsdp_1'=8,'fsdp_2'=4] {'z_hi','core'}, dimensions={0}, use_global_device_ids=true | all-gather | bytes 1003520 | tf_op jit(solution)/shard_map/all_gather | solution.py:53
  63.5 0.5 fusion.18
  64.0 0.1 slice.44
  64.1 0.1 fusion.12
  64.3 0.1 fusion.13
  64.4 0.0 copy-start.6
  64.4 0.8 %pad_maximum_fusion = f32[14,7168]{1,0:T(8,128)} fusion(f32[14,1792]{1,0:T(8,128)S(1)} %bitcast.57, f32[14,1792]{1,0:T(8,128)S(1)} %bitcast.56, f32[14,1792]{1,0:T(8,128)S(1)} %get-tuple-element.24, f32[14,1792]{1,0:T(8,128)S(1)} %get-tuple-element.17), kind=kLoop, calls=%fused_computation.4 | loop fusion | flops 301056 | bytes 802816 | tf_op jit(solution)/shard_map/concatenate | solution.py:54
  65.2 0.7 fusion.7
  66.7 0.1 copy.114
  66.8 0.1 copy.115
  67.0 0.3 reduce_sum.19
  67.3 0.6 fusion.19
  69.3 8.1 %maximum_add_fusion = (f32[1,14,7168]{2,0,1:T(1,128)}, f32[1,14,7168]{2,0,1:T(1,128)}, f32[1,14,7168]{2,0,1:T(1,128)}) fusion(f32[1,14,1792]{2,0,1:T(1,128)S(1)} %bitcast.54, f32[1,14,1792]{2,0,1:T(1,128)S(1)} %bitcast.55, f32[1,14,1792]{2,0,1:T(1,128)S(1)} %copy.115, f32[1,14,1792]{2,0,1:T(1,128)S(1)} %copy.114, f32[1,14,7168]{2,0,1:T(1,128)S(1)} %copy-done.1, ...), kind=kLoop, calls=%fused_computation.8 | loop fusion | flops 3913728 | bytes 3211288 | tf_op jit(solution)/shard_map/add | solution.py:93
  (15 shorter events, 0.1 us)
Async XLA Ops:
  2.3 27.7 %copy-start = (f32[14,7168]{1,0:T(8,128)S(1)}, f32[14,7168]{1,0:T(8,128)}, u32[]{:S(2)}) copy-start(f32[14,7168]{1,0:T(8,128)} %param.8) | copy-start | bytes 1204228
  4.0 63.0 %all-to-all-start = ((f32[256,1,2]{2,1,0:T(1,128)}), f32[256,1,2]{2,1,0:T(1,128)S(1)}, u32[]{:S(2)}, u32[]{:S(2)}) async-start(f32[256,1,2]{2,1,0:T(1,128)} %broadcast_in_dim.2), calls=%async_computation | async-start | bytes 262144 | tf_op jit(solution)/shard_map/all_to_all | solution.py:20
  30.0 1.0 %copy-start.1 = (f32[1,14,7168]{2,0,1:T(1,128)S(1)}, f32[1,14,7168]{2,0,1:T(1,128)}, u32[]{:S(2)}) copy-start(f32[1,14,7168]{2,0,1:T(1,128)} %param.10) | copy-start | bytes 1204228
  35.3 0.9 %copy-start.4 = (f32[14,1792]{1,0:T(8,128)S(1)}, f32[14,1792]{1,0:T(8,128)}, u32[]{:S(2)}) copy-start(f32[14,1792]{1,0:T(8,128)} %param.9) | copy-start | bytes 301060
  64.4 4.9 %copy-start.6 = (f32[1,14,7168]{2,0,1:T(1,128)S(1)}, f32[1,14,7168]{2,0,1:T(1,128)}, u32[]{:S(2)}) copy-start(f32[1,14,7168]{2,0,1:T(1,128)} %param.12) | copy-start | bytes 1204228
  65.2 4.1 %copy-start.5 = (f32[1,14,7168]{2,0,1:T(1,128)S(1)}, f32[1,14,7168]{2,0,1:T(1,128)}, u32[]{:S(2)}) copy-start(f32[1,14,7168]{2,0,1:T(1,128)} %param.11) | copy-start | bytes 1204228
  66.7 2.6 %copy-start.3 = (bf16[1,14,7168]{2,1,0:T(8,128)(2,1)S(1)}, bf16[1,14,7168]{2,1,0:T(8,128)(2,1)}, u32[]{:S(2)}) copy-start(bf16[1,14,7168]{2,1,0:T(8,128)(2,1)} %param.14) | copy-start | bytes 602116
  66.8 2.5 %copy-start.2 = (bf16[1,14,7168]{2,1,0:T(8,128)(2,1)S(1)}, bf16[1,14,7168]{2,1,0:T(8,128)(2,1)}, u32[]{:S(2)}) copy-start(bf16[1,14,7168]{2,1,0:T(8,128)(2,1)} %param.13) | copy-start | bytes 602116

commit v12 on v7

--- a/solution.py
+++ b/solution.py
@@ -3,6 +3,7 @@
 import jax
 import jax.numpy as jnp
 from jax import lax
+from jax.experimental.layout import Layout, with_layout_constraint
 from jax.sharding import Mesh
 from jax.sharding import PartitionSpec as P
 
@@ -96,7 +97,11 @@
     )
     next_anchor, next_momentum = outer_update(anchor, momentum, inner_weight)
     next_inner = (next_anchor + (weight - inner_weight[0]))[None]
-    return (next_anchor, next_momentum, next_inner, moment_one[None], moment_two[None])
+    stored = Layout(major_to_minor=(1, 0, 2))
+    next_inner, moment_one, moment_two = (
+        with_layout_constraint(x, stored) for x in (next_inner, moment_one[None], moment_two[None])
+    )
+    return (next_anchor, next_momentum, next_inner, moment_one, moment_two)
 
 
 def solution(mesh):

time: 73.4 us -> 78.1 us (1.064)
  other arithmetic: 4.66 us -> 12.4 us
  local copies, waits for them, and re-layouts: 9.34 us -> 6.11 us
    add x1, other arithmetic: 0.84 us -> 7.22 us  [on_device(): next_inner = (next_anchor + (weight - inner_weight[0]))[None]]
    unnamed x17 -> x14, local copies, waits for them, and re-layouts: 4.97 us -> 1.47 us
    convert_element_type x1, other arithmetic: 0.03 us -> 1.67 us  [inner_steps(): grad_two = grad_second[0].astype(jnp.float32)]
    convert_element_type x1 -> x0, other arithmetic: 1.01 us -> none  [inner_steps(): grad_one = grad_first[0].astype(jnp.float32)]
where the time goes in v12:
time: 78.1 us; the launch traced here: 77.8 us
  blocking collectives  30.1 us (39%)
  starting transfers between devices  26 us (33%)
  other arithmetic  12.4 us (16%)
  local copies, waits for them, and re-layouts  6.11 us (8%)
  between operations  3.16 us (4%)
    all_gather x1, blocking collectives, outer_update(): lax.all_gather(payload, REP, axis=0, tiled=False)  27.1 us
    all_to_all x1, starting transfers between devices, all_summed(): return lax.all_to_all(spread, axes, 0, 0, tiled=False).sum(axis=0)  26 us
    add x1, other arithmetic, on_device(): next_inner = (next_anchor + (weight - inner_weight[0]))[None]  7.22 us
    all_gather x1, blocking collectives, outer_update(): lax.all_gather(given, 'core', axis=0, tiled=False)  2.96 us
    reshape x2, local copies, waits for them, and re-layouts, outer_update(): next_anchor = jnp.stack([jnp.stack([every[h, c, :, 0] - 0.3325 * every[1...  1.69 us
    convert_element_type x1, other arithmetic, inner_steps(): grad_two = grad_second[0].astype(jnp.float32)  1.67 us
  transfers between devices with their start and end apart: 1, of which 0 were waited for; matrix products, arithmetic and copies ran while one was open for 7% of the time, Pallas kernels for 0%

profile of v12, /device:TPU:121, one launch (start us, length us, event | category | flops | bytes accessed | tf_op | source)
XLA Modules:
  0.0 77.8 jit_solution(3258269672714706112)
XLA Ops:
  0.6 1.7 %copy_convert_fusion = (f32[1,14,7168]{2,0,1:T(1,128)S(1)}, f32[1,14,7168]{2,0,1:T(1,128)S(1)}) fusion(bf16[1,14,7168]{2,1,0:T(8,128)(2,1)} %param.14, bf16[1,14,7168]{2,1,0:T(8,128)(2,1)} %param.13), kind=kLoop, calls=%fused_computation.8 | loop fusion | flops 200704 | bytes 1204224 | tf_op jit(solution)/shard_map/convert_element_type | solution.py:74
  2.3 0.0 copy-start
  2.3 0.9 %fusion = f32[2]{0:T(128)S(1)} fusion(f32[1,14,7168]{2,0,1:T(1,128)S(1)} %get-tuple-element.20, f32[1,14,7168]{2,0,1:T(1,128)S(1)} %get-tuple-element.21), kind=kLoop, calls=%fused_computation.1 | loop fusion | flops 602110 | bytes 802824 | tf_op jit(solution)/shard_map/reduce_sum | solution.py:76
  3.3 0.7 broadcast_in_dim.2
  4.0 26.0 %all-to-all-start = ((f32[256,1,2]{2,1,0:T(1,128)}), f32[256,1,2]{2,1,0:T(1,128)S(1)}, u32[]{:S(2)}, u32[]{:S(2)}) async-start(f32[256,1,2]{2,1,0:T(1,128)} %broadcast_in_dim.2), calls=%async_computation | async-start | bytes 262144 | tf_op jit(solution)/shard_map/all_to_all | solution.py:21
  30.0 0.0 copy-start.1
  30.1 0.3 reshape.163
  30.4 0.6 copy-done.1
  31.0 0.1 bitcast_subtract_fusion
  31.1 0.3 reshape.164
  31.5 0.4 constant_dynamic-slice_fusion.2
  31.8 0.1 copy.67
  32.0 3.0 %all-gather = f32[28,2,1,1792]{3,1,2,0:T(2,128)S(1)} all-gather(f32[14,2,1,1792]{3,1,2,0:T(2,128)S(1)} %copy.67), channel_id=2, replica_groups=mesh['z_hi'=2,'core'=2,'fsdp_0'=8,'fsdp_1'=8,'fsdp_2'=4] {'core'}, dimensions={0}, use_global_device_ids=true | all-gather | bytes 602112 | tf_op jit(solution)/shard_map/all_gather | solution.py:45
  34.9 0.1 bitcast_add_fusion
  35.1 0.2 constant_dynamic-slice_fusion.1
  35.3 0.0 copy-start.4
  35.3 0.1 constant_dynamic-slice_fusion.4
  35.4 0.8 %copy-done.4 = f32[14,1792]{1,0:T(8,128)S(1)} copy-done((f32[14,1792]{1,0:T(8,128)S(1)}, f32[14,1792]{1,0:T(8,128)}, u32[]{:S(2)}) %copy-start.4) | copy-done | bytes 100376
  36.2 0.1 stack.31
  36.3 0.2 pad_maximum_fusion.1
  36.5 27.1 %all-gather.1 = f32[56,2,1792]{2,1,0:T(2,128)S(1)} all-gather(f32[14,2,1792]{2,1,0:T(2,128)S(1)} %pad_maximum_fusion.1), channel_id=3, replica_groups=mesh['z_hi'=2,'core'=2,'fsdp_0'=8,'fsdp_1'=8,'fsdp_2'=4] {'z_hi','core'}, dimensions={0}, use_global_device_ids=true | all-gather | bytes 1003520 | tf_op jit(solution)/shard_map/all_gather | solution.py:54
  63.6 0.6 fusion.13
  64.2 0.1 slice.44
  64.3 0.7 fusion.7
  65.0 0.4 maximum_bitcast_fusion
  65.4 0.2 pad_maximum_fusion
  66.4 0.6 reshape.167
  67.0 0.0 copy-start.2
  67.1 1.1 %reshape.166 = f32[14,7168]{1,0:T(8,128)} reshape(f32[14,2,2,1792]{3,2,1,0:T(2,128)S(1)} %copy.69) | data formatting | bytes 802816 | tf_op jit(solution)/shard_map/reshape | solution.py:63
  68.2 0.3 reduce_sum.19
  68.4 0.6 fusion.18
  70.5 7.2 %subtract_add_fusion = (f32[1,14,7168]{2,0,1:T(1,128)}, f32[1,14,7168]{2,0,1:T(1,128)}, f32[1,14,7168]{2,0,1:T(1,128)}) fusion(f32[1,14,7168]{2,0,1:T(1,128)S(1)} %reshape.167, f32[1,14,7168]{2,0,1:T(1,128)S(1)} %copy-done.1, f32[]{:T(128)} %bitcast.18, f32[]{:T(128)} %bitcast.17, f32[]{:T(128)} %bitcast.15, f32[]{:T(128)} %bitcast.14, ...), kind=kLoop, calls=%fused_computation.10 | loop fusion | flops 3612672 | bytes 3211288 | tf_op jit(solution)/shard_map/add | solution.py:99
  (12 shorter events, 0.1 us)
Async XLA Ops:
  2.3 27.7 %copy-start = (f32[14,7168]{1,0:T(8,128)S(1)}, f32[14,7168]{1,0:T(8,128)}, u32[]{:S(2)}) copy-start(f32[14,7168]{1,0:T(8,128)} %param.8) | copy-start | bytes 1204228
  4.0 64.2 %all-to-all-start = ((f32[256,1,2]{2,1,0:T(1,128)}), f32[256,1,2]{2,1,0:T(1,128)S(1)}, u32[]{:S(2)}, u32[]{:S(2)}) async-start(f32[256,1,2]{2,1,0:T(1,128)} %broadcast_in_dim.2), calls=%async_computation | async-start | bytes 262144 | tf_op jit(solution)/shard_map/all_to_all | solution.py:21
  30.0 1.0 %copy-start.1 = (f32[1,14,7168]{2,0,1:T(1,128)S(1)}, f32[1,14,7168]{2,0,1:T(1,128)}, u32[]{:S(2)}) copy-start(f32[1,14,7168]{2,0,1:T(1,128)} %param.10) | copy-start | bytes 1204228
  35.3 0.9 %copy-start.4 = (f32[14,1792]{1,0:T(8,128)S(1)}, f32[14,1792]{1,0:T(8,128)}, u32[]{:S(2)}) copy-start(f32[14,1792]{1,0:T(8,128)} %param.9) | copy-start | bytes 301060
  66.4 4.1 %copy-start.6 = (f32[1,14,7168]{2,0,1:T(1,128)S(1)}, f32[1,14,7168]{2,0,1:T(1,128)}, u32[]{:S(2)}) copy-start(f32[1,14,7168]{2,0,1:T(1,128)} %param.12) | copy-start | bytes 1204228
  67.0 3.5 %copy-start.2 = (bf16[1,14,7168]{2,1,0:T(8,128)(2,1)S(1)}, bf16[1,14,7168]{2,1,0:T(8,128)(2,1)}, u32[]{:S(2)}) copy-start(bf16[1,14,7168]{2,1,0:T(8,128)(2,1)} %param.13) | copy-start | bytes 602116
  67.0 3.5 %copy-start.3 = (bf16[1,14,7168]{2,1,0:T(8,128)(2,1)S(1)}, bf16[1,14,7168]{2,1,0:T(8,128)(2,1)}, u32[]{:S(2)}) copy-start(bf16[1,14,7168]{2,1,0:T(8,128)(2,1)} %param.14) | copy-start | bytes 602116
  67.1 3.5 %copy-start.5 = (f32[1,14,7168]{2,0,1:T(1,128)S(1)}, f32[1,14,7168]{2,0,1:T(1,128)}, u32[]{:S(2)}) copy-start(f32[1,14,7168]{2,0,1:T(1,128)} %param.11) | copy-start | bytes 1204228

commit v13 on v7

--- a/solution.py
+++ b/solution.py
@@ -73,7 +73,7 @@
     grad_two = grad_second[0].astype(jnp.float32)
     both_grads = jnp.stack([grad_one, grad_two])
     squares = jnp.sum(both_grads * both_grads, axis=(1, 2))
-    norm_one, norm_two = all_summed(squares, FSDP)
+    norm_one, norm_two = all_summed(all_summed(squares, ("fsdp_0", "fsdp_2")), ("fsdp_1",))
     weight, moment_one, moment_two = adam_apply(
         inner_weight[0],
         first_moment[0],

time: 73.4 us -> 85.3 us (1.16)
  the two profiles are of different devices: /device:TPU:121 before, /device:TPU:2 now
where the time goes in v13:
time: 85.3 us; the launch traced here: 85 us
  starting transfers between devices  36.6 us (43%)
  blocking collectives  20.6 us (24%)
  waiting for transfers between devices  10.3 us (12%)
  local copies, waits for them, and re-layouts  9.83 us (12%)
  other arithmetic  4.44 us (5%)
  between operations  3.18 us (4%)
    all_to_all x2, starting transfers between devices, all_summed(): return lax.all_to_all(spread, axes, 0, 0, tiled=False).sum(axis=0)  36.6 us
    all_gather x1, blocking collectives, outer_update(): lax.all_gather(payload, REP, axis=0, tiled=False)  18.5 us
    all_to_all x2, waiting for transfers between devices, all_summed(): return lax.all_to_all(spread, axes, 0, 0, tiled=False).sum(axis=0)  10.3 us
    unnamed x17, local copies, waits for them, and re-layouts  4.97 us
    all_gather x1, blocking collectives, outer_update(): lax.all_gather(given, 'core', axis=0, tiled=False)  2.09 us
  transfers between devices with their start and end apart: 2, of which 1 were waited for; matrix products, arithmetic and copies ran while one was open for 6% of the time, Pallas kernels for 0%

profile of v13, /device:TPU:2, one launch (start us, length us, event | category | flops | bytes accessed | tf_op | source)
XLA Modules:
  0.0 85.0 jit_solution(17073025084023958679)
XLA Ops:
  0.6 1.0 %convert_element_type.22 = f32[1,14,7168]{2,1,0:T(8,128)S(1)} convert(bf16[1,14,7168]{2,1,0:T(8,128)(2,1)} %param.13) | non-fusion elementwise | flops 100352 | bytes 602112 | tf_op jit(solution)/shard_map/convert_element_type | solution.py:72
  1.7 0.2 fusion
  2.0 0.6 broadcast_in_dim.4
  2.6 16.7 %all-to-all-start = ((f32[32,1,2]{2,1,0:T(1,128)}), f32[32,1,2]{2,1,0:T(1,128)S(1)}, u32[]{:S(2)}, u32[]{:S(2)}) async-start(f32[32,1,2]{2,1,0:T(1,128)} %broadcast_in_dim.4), calls=%async_computation | async-start | bytes 32768 | tf_op jit(solution)/shard_map/all_to_all | solution.py:20
  19.9 0.3 reshape.169
  20.3 0.6 copy-done.1
  20.9 0.1 fusion.1
  21.0 0.3 reshape.170
  21.4 0.4 constant_dynamic-slice_fusion.2
  21.7 0.1 copy.90
  21.8 2.1 %all-gather = f32[28,2,1,1792]{3,1,2,0:T(2,128)S(1)} all-gather(f32[14,2,1,1792]{3,1,2,0:T(2,128)S(1)} %copy.90), channel_id=2, replica_groups=mesh['z_hi'=2,'core'=2,'fsdp_0'=8,'fsdp_1'=8,'fsdp_2'=4] {'core'}, dimensions={0}, use_global_device_ids=true | all-gather | bytes 602112 | tf_op jit(solution)/shard_map/all_gather | solution.py:44
  23.9 0.1 bitcast_add_fusion
  24.1 0.2 constant_dynamic-slice_fusion.1
  24.3 0.1 constant_dynamic-slice_fusion.4
  24.4 0.8 copy-done.4
  25.3 0.2 pad_maximum_fusion.1
  25.5 18.5 %all-gather.1 = f32[56,2,1792]{2,1,0:T(2,128)S(1)} all-gather(f32[14,2,1792]{2,1,0:T(2,128)S(1)} %pad_maximum_fusion.1), channel_id=3, replica_groups=mesh['z_hi'=2,'core'=2,'fsdp_0'=8,'fsdp_1'=8,'fsdp_2'=4] {'z_hi','core'}, dimensions={0}, use_global_device_ids=true | all-gather | bytes 1003520 | tf_op jit(solution)/shard_map/all_gather | solution.py:53
  44.0 0.6 fusion.18
  44.6 0.1 slice.44
  44.7 0.7 fusion.12
  45.5 0.4 maximum_bitcast_fusion
  45.8 0.2 pad_maximum_fusion
  46.2 0.3 reshape.173
  46.6 1.1 %reshape.172 = f32[14,7168]{1,0:T(8,128)} reshape(f32[14,2,2,1792]{3,2,1,0:T(2,128)S(1)} %copy.92) | data formatting | bytes 802816 | tf_op jit(solution)/shard_map/reshape | solution.py:62
  47.7 0.6 broadcast_in_dim.5
  48.3 19.9 %all-to-all-start.1 = ((f32[8,1,2]{2,1,0:T(1,128)}), f32[8,1,2]{2,1,0:T(1,128)S(1)}, u32[]{:S(2)}, u32[]{:S(2)}) async-start(f32[8,1,2]{2,1,0:T(1,128)} %broadcast_in_dim.5), calls=%async_computation.1 | async-start | bytes 8192 | tf_op jit(solution)/shard_map/all_to_all | solution.py:20
  68.2 10.3 %all-to-all-done.1 = f32[8,1,2]{2,1,0:T(1,128)S(1)} async-done(((f32[8,1,2]{2,1,0:T(1,128)}), f32[8,1,2]{2,1,0:T(1,128)S(1)}, u32[]{:S(2)}, u32[]{:S(2)}) %all-to-all-start.1) | async-done | bytes 96 | tf_op jit(solution)/shard_map/all_to_all | solution.py:20
  78.6 0.6 fusion.22
  80.6 0.8 fusion.6
  81.5 1.2 %copy.104 = f32[1,14,7168]{2,0,1:T(1,128)} copy(f32[1,14,7168]{2,1,0:T(8,128)S(1)} %get-tuple-element.30) | data formatting | bytes 802816
  82.6 1.2 %copy.102 = f32[1,14,7168]{2,0,1:T(1,128)} copy(f32[1,14,7168]{2,1,0:T(8,128)S(1)} %get-tuple-element.31) | data formatting | bytes 802816
  83.8 1.2 %copy.103 = f32[1,14,7168]{2,0,1:T(1,128)} copy(f32[1,14,7168]{2,1,0:T(8,128)S(1)} %get-tuple-element.32) | data formatting | bytes 802816
  (20 shorter events, 0.3 us)
Async XLA Ops:
  0.6 1.0 %copy-start.2 = (bf16[1,14,7168]{2,1,0:T(8,128)(2,1)S(1)}, bf16[1,14,7168]{2,1,0:T(8,128)(2,1)}, u32[]{:S(2)}) copy-start(bf16[1,14,7168]{2,1,0:T(8,128)(2,1)} %param.14) | copy-start | bytes 602116
  1.7 18.2 %copy-start = (f32[14,7168]{1,0:T(8,128)S(1)}, f32[14,7168]{1,0:T(8,128)}, u32[]{:S(2)}) copy-start(f32[14,7168]{1,0:T(8,128)} %param.8) | copy-start | bytes 1204228
  2.6 45.1 %all-to-all-start = ((f32[32,1,2]{2,1,0:T(1,128)}), f32[32,1,2]{2,1,0:T(1,128)S(1)}, u32[]{:S(2)}, u32[]{:S(2)}) async-start(f32[32,1,2]{2,1,0:T(1,128)} %broadcast_in_dim.4), calls=%async_computation | async-start | bytes 32768 | tf_op jit(solution)/shard_map/all_to_all | solution.py:20
  19.9 1.0 %copy-start.1 = (f32[1,14,7168]{2,0,1:T(1,128)S(1)}, f32[1,14,7168]{2,0,1:T(1,128)}, u32[]{:S(2)}) copy-start(f32[1,14,7168]{2,0,1:T(1,128)} %param.10) | copy-start | bytes 1204228
  24.3 0.9 %copy-start.4 = (f32[14,1792]{1,0:T(8,128)S(1)}, f32[14,1792]{1,0:T(8,128)}, u32[]{:S(2)}) copy-start(f32[14,1792]{1,0:T(8,128)} %param.9) | copy-start | bytes 301060
  46.2 34.4 %copy-start.6 = (f32[1,14,7168]{2,0,1:T(1,128)S(1)}, f32[1,14,7168]{2,0,1:T(1,128)}, u32[]{:S(2)}) copy-start(f32[1,14,7168]{2,0,1:T(1,128)} %param.11) | copy-start | bytes 1204228
  46.5 34.1 %copy-start.3 = (bf16[1,14,7168]{2,1,0:T(8,128)(2,1)S(1)}, bf16[1,14,7168]{2,1,0:T(8,128)(2,1)}, u32[]{:S(2)}) copy-start(bf16[1,14,7168]{2,1,0:T(8,128)(2,1)} %param.13) | copy-start | bytes 602116
  46.5 34.1 %copy-start.5 = (f32[1,14,7168]{2,0,1:T(1,128)S(1)}, f32[1,14,7168]{2,0,1:T(1,128)}, u32[]{:S(2)}) copy-start(f32[1,14,7168]{2,0,1:T(1,128)} %param.12) | copy-start | bytes 1204228
  48.3 30.2 %all-to-all-start.1 = ((f32[8,1,2]{2,1,0:T(1,128)}), f32[8,1,2]{2,1,0:T(1,128)S(1)}, u32[]{:S(2)}, u32[]{:S(2)}) async-start(f32[8,1,2]{2,1,0:T(1,128)} %broadcast_in_dim.5), calls=%async_computation.1 | async-start | bytes 8192 | tf_op jit(solution)/shard_map/all_to_all | solution.py:20

commit v14 on v7

--- a/solution.py
+++ b/solution.py
@@ -69,10 +69,11 @@
 
 def inner_steps(inner_weight, first_moment, second_moment, grad_first, grad_second, outer_step):
     base_step = 2 * outer_step[0]
+    both_grads = jnp.concatenate([grad_first, grad_second]).astype(jnp.float32)
+    squares = jnp.sum(both_grads * both_grads, axis=(1, 2))
+    grad_first, grad_second = lax.optimization_barrier((grad_first, grad_second))
     grad_one = grad_first[0].astype(jnp.float32)
     grad_two = grad_second[0].astype(jnp.float32)
-    both_grads = jnp.stack([grad_one, grad_two])
-    squares = jnp.sum(both_grads * both_grads, axis=(1, 2))
     norm_one, norm_two = all_summed(squares, FSDP)
     weight, moment_one, moment_two = adam_apply(
         inner_weight[0],

time: 73.4 us -> 73.5 us (level)
    reduce_sum x1, other arithmetic: 0.23 us -> 1.36 us  [inner_steps(): squares = jnp.sum(both_grads * both_grads, axis=(1, 2))]
    convert_element_type x2 -> x0, other arithmetic: 1.04 us -> none  [the longest x1 1.01 us: inner_steps(): grad_one = grad_first[0].astype(jnp.float32)]
where the time goes in v14:
time: 73.5 us; the launch traced here: 73.2 us
  blocking collectives  29.9 us (41%)
  starting transfers between devices  26 us (35%)
  local copies, waits for them, and re-layouts  9.32 us (13%)
  other arithmetic  4.74 us (6%)
  between operations  3.16 us (4%)
    all_gather x1, blocking collectives, outer_update(): lax.all_gather(payload, REP, axis=0, tiled=False)  27 us
    all_to_all x1, starting transfers between devices, all_summed(): return lax.all_to_all(spread, axes, 0, 0, tiled=False).sum(axis=0)  26 us
    unnamed x17, local copies, waits for them, and re-layouts  4.95 us
    all_gather x1, blocking collectives, outer_update(): lax.all_gather(given, 'core', axis=0, tiled=False)  2.96 us
  transfers between devices with their start and end apart: 1, of which 0 were waited for; matrix products, arithmetic and copies ran while one was open for 7% of the time, Pallas kernels for 0%

profile of v14, /device:TPU:121, one launch (start us, length us, event | category | flops | bytes accessed | tf_op | source)
XLA Modules:
  0.0 73.2 jit_solution(14514968793124288831)
XLA Ops:
  0.6 1.4 %multiply_reduce_fusion = f32[2]{0:T(128)S(1)} fusion(bf16[1,14,7168]{2,1,0:T(8,128)(2,1)} %param.14, bf16[1,14,7168]{2,1,0:T(8,128)(2,1)} %param.13), kind=kLoop, calls=%fused_computation | loop fusion | flops 802814 | bytes 401416 | tf_op jit(solution)/shard_map/reduce_sum | solution.py:73
  2.0 0.7 broadcast_in_dim.2
  2.7 26.0 %all-to-all-start = ((f32[256,1,2]{2,1,0:T(1,128)}), f32[256,1,2]{2,1,0:T(1,128)S(1)}, u32[]{:S(2)}, u32[]{:S(2)}) async-start(f32[256,1,2]{2,1,0:T(1,128)} %broadcast_in_dim.2), calls=%async_computation | async-start | bytes 262144 | tf_op jit(solution)/shard_map/all_to_all | solution.py:20
  28.8 0.0 copy-start.1
  28.8 0.3 reshape.163
  29.1 0.6 copy-done.1
  29.8 0.1 fusion
  29.9 0.3 reshape.164
  30.2 0.4 constant_dynamic-slice_fusion.2
  30.6 0.1 copy.90
  30.7 3.0 %all-gather = f32[28,2,1,1792]{3,1,2,0:T(2,128)S(1)} all-gather(f32[14,2,1,1792]{3,1,2,0:T(2,128)S(1)} %copy.90), channel_id=2, replica_groups=mesh['z_hi'=2,'core'=2,'fsdp_0'=8,'fsdp_1'=8,'fsdp_2'=4] {'core'}, dimensions={0}, use_global_device_ids=true | all-gather | bytes 602112 | tf_op jit(solution)/shard_map/all_gather | solution.py:44
  33.7 0.1 bitcast_add_fusion
  33.8 0.2 constant_dynamic-slice_fusion.1
  34.0 0.1 constant_dynamic-slice_fusion.4
  34.1 0.8 %copy-done.4 = f32[14,1792]{1,0:T(8,128)S(1)} copy-done((f32[14,1792]{1,0:T(8,128)S(1)}, f32[14,1792]{1,0:T(8,128)}, u32[]{:S(2)}) %copy-start.4) | copy-done | bytes 100376
  34.9 0.1 stack.26
  35.0 0.2 pad_maximum_fusion.1
  35.2 27.0 %all-gather.1 = f32[56,2,1792]{2,1,0:T(2,128)S(1)} all-gather(f32[14,2,1792]{2,1,0:T(2,128)S(1)} %pad_maximum_fusion.1), channel_id=3, replica_groups=mesh['z_hi'=2,'core'=2,'fsdp_0'=8,'fsdp_1'=8,'fsdp_2'=4] {'z_hi','core'}, dimensions={0}, use_global_device_ids=true | all-gather | bytes 1003520 | tf_op jit(solution)/shard_map/all_gather | solution.py:53
  62.2 0.6 fusion.17
  62.8 0.1 slice.44
  62.9 0.7 fusion.11
  63.6 0.4 maximum_bitcast_fusion
  64.0 0.2 pad_maximum_fusion
  65.0 0.3 reshape.167
  65.3 0.0 copy-start.2
  65.4 1.1 %reshape.166 = f32[14,7168]{1,0:T(8,128)} reshape(f32[14,2,2,1792]{3,2,1,0:T(2,128)S(1)} %copy.92) | data formatting | bytes 802816 | tf_op jit(solution)/shard_map/reshape | solution.py:62
  66.5 0.3 reduce_sum.19
  66.8 0.6 fusion.21
  68.8 0.8 %fusion.5 = (f32[1,14,7168]{2,1,0:T(8,128)S(1)}, f32[1,14,7168]{2,1,0:T(8,128)S(1)}, f32[1,14,7168]{2,1,0:T(8,128)S(1)}) fusion(bf16[1,14,7168]{2,1,0:T(8,128)(2,1)S(1)} %copy-done.2, f32[]{:T(128)} %bitcast.16, bf16[1,14,7168]{2,1,0:T(8,128)(2,1)S(1)} %copy-done.3, f32[1,14,7168]{2,0,1:T(1,128)S(1)} %copy-done.5, f32[]{:T(128)} %bitcast.13, ...), kind=kLoop, calls=%fused_computation.12 | loop fusion | flops 3612672 | bytes 3211288 | tf_op jit(solution)/shard_map/add | solution.py:27
  69.7 1.2 %copy.103 = f32[1,14,7168]{2,0,1:T(1,128)} copy(f32[1,14,7168]{2,1,0:T(8,128)S(1)} %get-tuple-element.34) | data formatting | bytes 802816
  70.9 1.2 %copy.101 = f32[1,14,7168]{2,0,1:T(1,128)} copy(f32[1,14,7168]{2,1,0:T(8,128)S(1)} %get-tuple-element.35) | data formatting | bytes 802816
  72.0 1.2 %copy.102 = f32[1,14,7168]{2,0,1:T(1,128)} copy(f32[1,14,7168]{2,1,0:T(8,128)S(1)} %get-tuple-element.36) | data formatting | bytes 802816
  (14 shorter events, 0.1 us)
Async XLA Ops:
  0.6 28.1 %copy-start = (f32[14,7168]{1,0:T(8,128)S(1)}, f32[14,7168]{1,0:T(8,128)}, u32[]{:S(2)}) copy-start(f32[14,7168]{1,0:T(8,128)} %param.8) | copy-start | bytes 1204228
  2.7 63.7 %all-to-all-start = ((f32[256,1,2]{2,1,0:T(1,128)}), f32[256,1,2]{2,1,0:T(1,128)S(1)}, u32[]{:S(2)}, u32[]{:S(2)}) async-start(f32[256,1,2]{2,1,0:T(1,128)} %broadcast_in_dim.2), calls=%async_computation | async-start | bytes 262144 | tf_op jit(solution)/shard_map/all_to_all | solution.py:20
  28.8 1.0 %copy-start.1 = (f32[1,14,7168]{2,0,1:T(1,128)S(1)}, f32[1,14,7168]{2,0,1:T(1,128)}, u32[]{:S(2)}) copy-start(f32[1,14,7168]{2,0,1:T(1,128)} %param.10) | copy-start | bytes 1204228
  34.0 0.9 %copy-start.4 = (f32[14,1792]{1,0:T(8,128)S(1)}, f32[14,1792]{1,0:T(8,128)}, u32[]{:S(2)}) copy-start(f32[14,1792]{1,0:T(8,128)} %param.9) | copy-start | bytes 301060
  65.0 3.8 %copy-start.6 = (f32[1,14,7168]{2,0,1:T(1,128)S(1)}, f32[1,14,7168]{2,0,1:T(1,128)}, u32[]{:S(2)}) copy-start(f32[1,14,7168]{2,0,1:T(1,128)} %param.11) | copy-start | bytes 1204228
  65.3 3.5 %copy-start.2 = (bf16[1,14,7168]{2,1,0:T(8,128)(2,1)S(1)}, bf16[1,14,7168]{2,1,0:T(8,128)(2,1)}, u32[]{:S(2)}) copy-start(bf16[1,14,7168]{2,1,0:T(8,128)(2,1)} %param.14) | copy-start | bytes 602116
  65.4 3.5 %copy-start.3 = (bf16[1,14,7168]{2,1,0:T(8,128)(2,1)S(1)}, bf16[1,14,7168]{2,1,0:T(8,128)(2,1)}, u32[]{:S(2)}) copy-start(bf16[1,14,7168]{2,1,0:T(8,128)(2,1)} %param.13) | copy-start | bytes 602116
  65.4 3.5 %copy-start.5 = (f32[1,14,7168]{2,0,1:T(1,128)S(1)}, f32[1,14,7168]{2,0,1:T(1,128)}, u32[]{:S(2)}) copy-start(f32[1,14,7168]{2,0,1:T(1,128)} %param.12) | copy-start | bytes 1204228
